TPU v7x, 512 devices: a whole 4x4x16 slice. The times are simulated.
512 devices in a mesh: dp: 16 (over z), expert: 32 (over x, y, core).
Axes of the slice: x: 4, y: 4, z: 16, core: 2. Of those that a mesh axis runs over, the one named last changes fastest.
Arguments:
- x_tokens: bfloat16 [65536, 2048], P(('dp', 'expert')), may hold values from -6 to 6
- grad_out: bfloat16 [65536, 2048], P(('dp', 'expert')), may hold values from -6 to 6
- expert_ids: int32 [65536, 2], P(('dp', 'expert')), may hold values from 0 to 31, all different within a row; in each aligned block of 128 rows (0 to 127, 128 to 255, ...) at most 10 rows name the same one
- route_probs: float32 [65536, 2], P(('dp', 'expert')), may hold values from 0.1 to 1
- w_gate: bfloat16 [32, 2048, 768], P('expert', 'dp'), may hold values from -0.125 to 0.125
- w_up: bfloat16 [32, 2048, 768], P('expert', 'dp'), may hold values from -0.125 to 0.125
- w_down: bfloat16 [32, 2048, 768], P('expert', 'dp'), may hold values from -0.21875 to 0.21875
Outputs:
- grad_x: bfloat16 [65536, 2048], P(('dp', 'expert'))
- grad_probs: bfloat16 [65536, 2], P(('dp', 'expert'))
- grad_w_down: bfloat16 [32, 2048, 768], P('expert', 'dp')
Inputs may be any that keep to these rules, and one draw needn't show every extreme that they name: `expert_ids`: each token names 2 different experts; among the 128 tokens of one device no expert is named by more than 10 routes, and in every draw some device names some expert exactly 10 times.
All inputs are finite; a program needn't handle non-finite values.
Results may differ from a plain program's by a relative error of at most 0.017.
Values may be sent and summed in bfloat16 or wider, within the bound.
No kernel may reach another device: no remote copies, remote signals or barrier semaphores. Data moves between devices by JAX's collectives and lax.ppermute only.
A program may use at most 64 MiB of HBM per device.

v0:
```python
import jax
import jax.numpy as jnp
from jax import lax
from jax.sharding import PartitionSpec as P


def per_device(x_tokens, grad_out, expert_ids, route_probs, w_gate, w_up, w_down):
    tok_count, model_width = x_tokens.shape
    top_count = expert_ids.shape[1]
    n_expert = lax.axis_size("expert")
    capacity = tok_count * top_count * 5 // (4 * n_expert)
    slot_count = n_expert * capacity
    routes = tok_count * top_count
    flat_ids = expert_ids.reshape(routes)
    onehot = (flat_ids[:, None] == jnp.arange(n_expert, dtype=jnp.int32)).astype(jnp.int32)
    route_rank = jnp.sum((jnp.cumsum(onehot, axis=0) - onehot) * onehot, axis=1)
    target = flat_ids * capacity + route_rank
    source = (
        jnp.full((slot_count,), routes, jnp.int32)
        .at[target]
        .set(jnp.arange(routes, dtype=jnp.int32))
    )
    token_of = jnp.where(source < routes, source // top_count, tok_count)
    x_padded = jnp.concatenate([x_tokens, jnp.zeros((1, model_width), jnp.bfloat16)], axis=0)
    dy_padded = jnp.concatenate([grad_out, jnp.zeros((1, model_width), jnp.bfloat16)], axis=0)
    p_padded = jnp.concatenate([route_probs.reshape(routes), jnp.zeros((1,), jnp.float32)]).astype(
        jnp.bfloat16
    )
    x_slots = x_padded[token_of].reshape(n_expert, capacity, model_width)
    dy_slots = dy_padded[token_of].reshape(n_expert, capacity, model_width)
    p_slots = p_padded[source].reshape(n_expert, capacity)
    arrived = (
        lax.all_to_all(x_slots, "expert", split_axis=0, concat_axis=0, tiled=True),
        lax.all_to_all(dy_slots, "expert", split_axis=0, concat_axis=0, tiled=True),
        lax.all_to_all(p_slots, "expert", split_axis=0, concat_axis=0, tiled=True),
    )
    in_rows = arrived[0].reshape(slot_count, model_width)
    dy_rows = arrived[1].reshape(slot_count, model_width)
    p_rows = arrived[2].reshape(slot_count).astype(jnp.float32)
    scaled = (p_rows[:, None] * dy_rows.astype(jnp.float32)).astype(jnp.bfloat16)
    gate_full, up_full = (
        lax.all_gather(w_gate, "dp", axis=1, tiled=True),
        lax.all_gather(w_up, "dp", axis=1, tiled=True),
    )
    gate_full = gate_full[0]
    up_full = up_full[0]
    gate_pre = jnp.dot(in_rows, gate_full, preferred_element_type=jnp.float32)
    up_pre = jnp.dot(in_rows, up_full, preferred_element_type=jnp.float32)
    gate_sig = jax.nn.sigmoid(gate_pre)
    gate_act = gate_pre * gate_sig
    hidden = (gate_act * up_pre).astype(jnp.bfloat16)
    piece_rows = lax.all_gather(w_down, "dp", axis=1, tiled=True)[0]
    out_piece = jnp.dot(hidden, piece_rows.T, preferred_element_type=jnp.float32)
    grad_sum = jnp.dot(scaled, piece_rows, preferred_element_type=jnp.float32)
    prob_sum = jnp.sum(dy_rows.astype(jnp.float32) * out_piece, axis=1)
    hidden_grad, prob_sum = (grad_sum, prob_sum)
    up_grad = (hidden_grad * gate_act).astype(jnp.bfloat16)
    gate_grad = (hidden_grad * up_pre * gate_sig * (1.0 + gate_pre * (1.0 - gate_sig))).astype(
        jnp.bfloat16
    )
    x_grad = (
        jnp.dot(gate_grad, gate_full.T, preferred_element_type=jnp.float32)
        + jnp.dot(up_grad, up_full.T, preferred_element_type=jnp.float32)
    ).astype(jnp.bfloat16)
    down_grad = lax.psum_scatter(
        lax.dot_general(
            scaled, hidden, (((0,), (0,)), ((), ())), preferred_element_type=jnp.float32
        ).astype(jnp.bfloat16),
        "dp",
        scatter_dimension=0,
        tiled=True,
    )
    grad_w_down = down_grad[None]
    returned = (
        lax.all_to_all(
            x_grad.reshape(n_expert, capacity, model_width),
            "expert",
            split_axis=0,
            concat_axis=0,
            tiled=True,
        ),
        lax.all_to_all(
            prob_sum.astype(jnp.bfloat16).reshape(n_expert, capacity),
            "expert",
            split_axis=0,
            concat_axis=0,
            tiled=True,
        ),
    )
    grad_slots = returned[0].reshape(slot_count, model_width)
    prob_slots = returned[1].reshape(slot_count)
    picked = grad_slots[target].astype(jnp.float32).reshape(tok_count, top_count, model_width)
    grad_x = jnp.sum(picked, axis=1).astype(jnp.bfloat16)
    grad_probs = prob_slots[target].reshape(tok_count, top_count)
    return (grad_x, grad_probs, grad_w_down)


def solution(mesh):
    return jax.shard_map(
        per_device,
        mesh=mesh,
        in_specs=(
            P(("dp", "expert"), None),
            P(("dp", "expert"), None),
            P(("dp", "expert"), None),
            P(("dp", "expert"), None),
            P("expert", "dp", None),
            P("expert", "dp", None),
            P("expert", "dp", None),
        ),
        out_specs=(P(("dp", "expert"), None), P(("dp", "expert"), None), P("expert", "dp", None)),
        check_vma=False,
    )
```

profile of v0, /device:TPU:4, one launch (start us, length us, event | category | flops | bytes accessed | tf_op | source)
XLA Modules:
  0.0 322.4 jit_solution(13100136976467206266)
XLA Ops:
  7.2 0.7 all-gather.8.cloned.1.call-update
  8.0 0.7 all-gather.6.cloned.1.call-update
  8.7 0.7 all-gather.4.cloned.1.call-update
  9.4 0.8 copy.18
  10.5 0.7 convert.9
  11.4 0.7 broadcast_multiply_fusion
  12.4 0.6 reduce-window.6
  13.0 0.2 slice_reduce_fusion
  13.3 1.4 scatter_custom_fusion
  14.8 2.5 gather_fusion
  17.3 0.7 all_to_all.25
  18.0 9.4 %all-to-all-start = ((bf16[32,1,10]{2,1,0:T(2,128)(2,1)}), bf16[32,1,10]{2,1,0:T(2,128)(2,1)S(1)}, u32[]{:S(2)}, u32[]{:S(2)}) async-start(bf16[32,1,10]{2,1,0:T(2,128)(2,1)} %all_to_all.25), calls=%async_computation | async-start | bytes 32768 | tf_op jit(solution)/shard_map/all_to_all | solution.py:35
  27.5 2.4 gather_fusion.2
  29.9 1.7 reshape.123
  31.6 1.1 all-to-all-done
  32.7 6.4 %all-to-all-start.2 = ((bf16[32,10,2048]{2,1,0:T(8,128)(2,1)}), bf16[32,10,2048]{2,1,0:T(8,128)(2,1)S(1)}, u32[]{:S(2)}, u32[]{:S(2)}) async-start(bf16[32,10,2048]{2,1,0:T(8,128)(2,1)} %reshape.123), calls=%async_computation.2 | async-start | bytes 4194304 | tf_op jit(solution)/shard_map/all_to_all | solution.py:33
  39.2 3.0 gather_fusion.1
  42.2 3.3 %reshape.122 = bf16[32,10,2048]{2,1,0:T(8,128)(2,1)} reshape(bf16[320,2048]{1,0:T(8,128)(2,1)} %gather_fusion.1) | data formatting | bytes 2621440 | tf_op jit(solution)/shard_map/reshape | solution.py:30
  45.6 19.5 %all-to-all-done.2 = bf16[32,10,2048]{2,1,0:T(8,128)(2,1)S(1)} async-done(((bf16[32,10,2048]{2,1,0:T(8,128)(2,1)}), bf16[32,10,2048]{2,1,0:T(8,128)(2,1)S(1)}, u32[]{:S(2)}, u32[]{:S(2)}) %all-to-all-start.2) | async-done | bytes 1310752 | tf_op jit(solution)/shard_map/all_to_all | solution.py:33
  65.0 7.7 %all-to-all-start.1 = ((bf16[32,10,2048]{2,1,0:T(8,128)(2,1)}), bf16[32,10,2048]{2,1,0:T(8,128)(2,1)}, u32[]{:S(2)}, u32[]{:S(2)}) async-start(bf16[32,10,2048]{2,1,0:T(8,128)(2,1)} %reshape.122), calls=%async_computation.1 | async-start | bytes 4194304 | tf_op jit(solution)/shard_map/all_to_all | solution.py:34
  72.7 0.2 reduce-scatter.2.cloned.1.call-start
  73.1 1.4 reshape.124
  74.5 24.1 %all-to-all-done.1 = bf16[32,10,2048]{2,1,0:T(8,128)(2,1)} async-done(((bf16[32,10,2048]{2,1,0:T(8,128)(2,1)}), bf16[32,10,2048]{2,1,0:T(8,128)(2,1)}, u32[]{:S(2)}, u32[]{:S(2)}) %all-to-all-start.1) | async-done | bytes 1310752 | tf_op jit(solution)/shard_map/all_to_all | solution.py:34
  98.6 2.5 reshape.130
  101.1 4.4 %fusion.2 = f32[320,768]{1,0:T(8,128)} fusion(bf16[320,2048]{1,0:T(8,128)(2,1)} %reshape.124, bf16[1,2048,768]{2,1,0:T(8,128)(2,1)} %all-gather.8.cloned.1.call-done), kind=kOutput, calls=%fused_computation.10 | convolution fusion | flops 1006632960 | bytes 5439488 | tf_op jit(solution)/shard_map/dot_general | solution.py:47
  105.6 58.7 %all-gather.6.cloned.1.call-done = bf16[1,2048,768]{2,1,0:T(8,128)(2,1)} async-done(((bf16[1,128,768]{2,1,0:T(8,128)(2,1)}), bf16[1,2048,768]{2,1,0:T(8,128)(2,1)}) %all-gather.6.cloned.1.call-update) | async-done | bytes 3145744 | tf_op jit(solution)/shard_map/all_gather | solution.py:43
  164.3 4.7 %multiply_convert_fusion.3 = (bf16[320,768]{1,0:T(8,128)(2,1)S(1)}, f32[320,768]{1,0:T(8,128)}) fusion(f32[320,768]{1,0:T(8,128)} %fusion.2, bf16[320,2048]{1,0:T(8,128)(2,1)} %reshape.124, bf16[1,2048,768]{2,1,0:T(8,128)(2,1)} %all-gather.6.cloned.1.call-done), kind=kOutput, calls=%fused_computation.26 | convolution fusion | flops 1008107520 | bytes 6914048 | tf_op jit(solution)/shard_map/dot_general | solution.py:48
  169.0 3.6 %convolution_convert_fusion = bf16[2048,768]{1,0:T(8,128)(2,1)} fusion(bf16[320,768]{1,0:T(8,128)(2,1)S(1)} %get-tuple-element.11, f32[320,2048]{1,0:T(8,128)S(1)} %reshape.130, f32[320]{0:T(512)S(1)} %reshape.131), kind=kOutput, calls=%fused_computation.7 | convolution fusion | flops 1009516544 | bytes 6259968 | tf_op jit(solution)/shard_map/dot_general | solution.py:66
  172.6 3.3 %multiply_convert_fusion = bf16[32,10,2048]{2,1,0:T(8,128)(2,1)} fusion(f32[32,10]{1,0:T(8,128)S(1)} %bitcast.54, bf16[32,10,2048]{2,1,0:T(8,128)(2,1)} %all-to-all-done.1), kind=kLoop, calls=%fused_computation.6 | loop fusion | flops 1966080 | bytes 2622720 | tf_op jit(solution)/shard_map/convert_element_type | solution.py:40
  175.9 3.6 %convert_element_type.80 = bf16[320,2048]{1,0:T(8,128)(2,1)} reshape(bf16[32,10,2048]{2,1,0:T(8,128)(2,1)} %multiply_convert_fusion) | data formatting | bytes 2621440 | tf_op jit(solution)/shard_map/convert_element_type | solution.py:40
  179.5 59.1 %all-gather.4.cloned.1.call-done = bf16[1,2048,768]{2,1,0:T(8,128)(2,1)} async-done(((bf16[1,128,768]{2,1,0:T(8,128)(2,1)}), bf16[1,2048,768]{2,1,0:T(8,128)(2,1)}) %all-gather.4.cloned.1.call-update) | async-done | bytes 3145744 | tf_op jit(solution)/shard_map/all_gather | solution.py:52
  238.7 3.2 fusion.21
  241.9 0.7 convert_element_type.96
  242.6 7.4 %all-to-all-start.4 = ((bf16[32,1,10]{2,1,0:T(2,128)(2,1)}), bf16[32,1,10]{2,1,0:T(2,128)(2,1)S(1)}, u32[]{:S(2)}, u32[]{:S(2)}) async-start(bf16[32,1,10]{2,1,0:T(2,128)(2,1)} %convert_element_type.96), calls=%async_computation.4 | async-start | bytes 32768 | tf_op jit(solution)/shard_map/all_to_all | solution.py:82
  250.1 3.6 %fusion.10 = f32[320,768]{1,0:T(8,128)S(1)} fusion(bf16[320,2048]{1,0:T(8,128)(2,1)} %convert_element_type.80, bf16[1,2048,768]{2,1,0:T(8,128)(2,1)} %all-gather.4.cloned.1.call-done), kind=kOutput, calls=%fused_computation.18 | convolution fusion | flops 1006632960 | bytes 5439488 | tf_op jit(solution)/shard_map/dot_general | solution.py:54
  253.8 1.3 fusion
  255.2 0.7 copy-done.3
  255.8 1.2 fusion.18
  257.0 1.6 reshape.125
  258.6 7.4 %all-to-all-start.3 = ((bf16[32,10,2048]{2,1,0:T(8,128)(2,1)}), bf16[32,10,2048]{2,1,0:T(8,128)(2,1)S(1)}, u32[]{:S(2)}, u32[]{:S(2)}) async-start(bf16[32,10,2048]{2,1,0:T(8,128)(2,1)} %reshape.125), calls=%async_computation.3 | async-start | bytes 4194304 | tf_op jit(solution)/shard_map/all_to_all | solution.py:75
  266.2 1.9 gather_fusion.4
  268.3 0.6 copy.23
  268.9 23.0 %all-to-all-done.3 = bf16[32,10,2048]{2,1,0:T(8,128)(2,1)S(1)} async-done(((bf16[32,10,2048]{2,1,0:T(8,128)(2,1)}), bf16[32,10,2048]{2,1,0:T(8,128)(2,1)S(1)}, u32[]{:S(2)}, u32[]{:S(2)}) %all-to-all-start.3) | async-done | bytes 1310752 | tf_op jit(solution)/shard_map/all_to_all | solution.py:75
  291.9 0.5 reshape.126
  292.4 1.4 gather_fusion.3
  293.8 0.7 gather.21
  294.5 3.6 %reduce_sum.34 = bf16[128,2048]{1,0:T(8,128)(2,1)} reduce(bf16[128,2,2048]{2,1,0:T(2,128)(2,1)S(1)} %gather.21, bf16[]{:T(256)} %constant.36.clone.1), dimensions={1}, to_apply=%region_4.5 | reduce | flops 262144 | bytes 1572866 | tf_op jit(solution)/shard_map/reduce_sum | solution.py:93
  298.1 17.8 %reduce-scatter.2.cloned.1.call-done = bf16[128,768]{1,0:T(8,128)(2,1)} async-done(((bf16[2048,768]{1,0:T(8,128)(2,1)}), bf16[128,768]{1,0:T(8,128)(2,1)}) %reduce-scatter.2.cloned.1.call-update) | async-done | bytes 196624 | tf_op jit(solution)/shard_map/reduce_scatter | solution.py:65
  (41 shorter events, 1.9 us)
Async XLA Ops:
  7.2 20.3 %copy-start = (bf16[128,2048]{1,0:T(8,128)(2,1)S(1)}, bf16[128,2048]{1,0:T(8,128)(2,1)}, u32[]{:S(2)}) copy-start(bf16[128,2048]{1,0:T(8,128)(2,1)} %param.7) | copy-start | bytes 1572868
  7.2 94.0 %all-gather.8.cloned.1.call-start = ((), (), s32[]{:S(2)}) async-start(), calls=%async_computation.8 | async-start | bytes 3342336 | tf_op jit(solution)/shard_map/all_gather | solution.py:42
  7.9 156.4 %all-gather.6.cloned.1.call-start = ((), (), s32[]{:S(2)}) async-start(), calls=%async_computation.7 | async-start | bytes 3342336 | tf_op jit(solution)/shard_map/all_gather | solution.py:43
  8.7 230.0 %all-gather.4.cloned.1.call-start = ((), (), s32[]{:S(2)}) async-start(), calls=%async_computation.6 | async-start | bytes 3342336 | tf_op jit(solution)/shard_map/all_gather | solution.py:52
  18.0 14.7 %all-to-all-start = ((bf16[32,1,10]{2,1,0:T(2,128)(2,1)}), bf16[32,1,10]{2,1,0:T(2,128)(2,1)S(1)}, u32[]{:S(2)}, u32[]{:S(2)}) async-start(bf16[32,1,10]{2,1,0:T(2,128)(2,1)} %all_to_all.25), calls=%async_computation | async-start | bytes 32768 | tf_op jit(solution)/shard_map/all_to_all | solution.py:35
  31.6 7.5 %copy-start.1 = (bf16[128,2048]{1,0:T(8,128)(2,1)S(1)}, bf16[128,2048]{1,0:T(8,128)(2,1)}, u32[]{:S(2)}) copy-start(bf16[128,2048]{1,0:T(8,128)(2,1)} %param.8) | copy-start | bytes 1572868
  32.7 32.4 %all-to-all-start.2 = ((bf16[32,10,2048]{2,1,0:T(8,128)(2,1)}), bf16[32,10,2048]{2,1,0:T(8,128)(2,1)S(1)}, u32[]{:S(2)}, u32[]{:S(2)}) async-start(bf16[32,10,2048]{2,1,0:T(8,128)(2,1)} %reshape.123), calls=%async_computation.2 | async-start | bytes 4194304 | tf_op jit(solution)/shard_map/all_to_all | solution.py:33
  65.0 33.6 %all-to-all-start.1 = ((bf16[32,10,2048]{2,1,0:T(8,128)(2,1)}), bf16[32,10,2048]{2,1,0:T(8,128)(2,1)}, u32[]{:S(2)}, u32[]{:S(2)}) async-start(bf16[32,10,2048]{2,1,0:T(8,128)(2,1)} %reshape.122), calls=%async_computation.1 | async-start | bytes 4194304 | tf_op jit(solution)/shard_map/all_to_all | solution.py:34
  72.7 243.2 %reduce-scatter.2.cloned.1.call-start = ((), (), s32[]{:S(2)}) async-start(), calls=%async_computation.9 | async-start | bytes 3342336 | tf_op jit(solution)/shard_map/reduce_scatter | solution.py:65
  242.6 16.0 %all-to-all-start.4 = ((bf16[32,1,10]{2,1,0:T(2,128)(2,1)}), bf16[32,1,10]{2,1,0:T(2,128)(2,1)S(1)}, u32[]{:S(2)}, u32[]{:S(2)}) async-start(bf16[32,1,10]{2,1,0:T(2,128)(2,1)} %convert_element_type.96), calls=%async_computation.4 | async-start | bytes 32768 | tf_op jit(solution)/shard_map/all_to_all | solution.py:82
  250.0 3.6 %copy-start.2 = (bf16[1,2048,768]{2,1,0:T(8,128)(2,1)S(1)}, bf16[1,2048,768]{2,1,0:T(8,128)(2,1)}, u32[]{:S(2)}) copy-start(bf16[1,2048,768]{2,1,0:T(8,128)(2,1)} %all-gather.8.cloned.1.call-done) | copy-start | bytes 9437188
  250.0 3.6 %copy-start.4 = (f32[320,768]{1,0:T(8,128)S(1)}, f32[320,768]{1,0:T(8,128)}, u32[]{:S(2)}) copy-start(f32[320,768]{1,0:T(8,128)} %fusion.2) | copy-start | bytes 2949124
  250.0 3.8 %copy-start.5 = (f32[320,768]{1,0:T(8,128)S(1)}, f32[320,768]{1,0:T(8,128)}, u32[]{:S(2)}) copy-start(f32[320,768]{1,0:T(8,128)} %get-tuple-element.12) | copy-start | bytes 2949124
  253.8 2.0 copy-start.3
  258.6 33.3 %all-to-all-start.3 = ((bf16[32,10,2048]{2,1,0:T(8,128)(2,1)}), bf16[32,10,2048]{2,1,0:T(8,128)(2,1)S(1)}, u32[]{:S(2)}, u32[]{:S(2)}) async-start(bf16[32,10,2048]{2,1,0:T(8,128)(2,1)} %reshape.125), calls=%async_computation.3 | async-start | bytes 4194304 | tf_op jit(solution)/shard_map/all_to_all | solution.py:75
Sparse Core Ops, SparseCore 0:
  10.1 79.8 all-gather.7
  92.0 72.2 all-gather.5
  166.4 72.2 all-gather.3
  241.9 73.9 reduce-scatter.1
where the time goes:
time: 323 us; the launch traced here: 322 us
  waiting for transfers between devices  205 us (63%)
  starting transfers between devices  38.7 us (12%)
  local copies, waits for them, and re-layouts  32.9 us (10%)
  matrix products  22.1 us (7%)
  between operations  14.1 us (4%)
  other arithmetic  9.22 us (3%)
    all_gather x1, waiting for transfers between devices, per_device(): piece_rows = lax.all_gather(w_down, 'dp', axis=1, tiled=True)[0]  59.1 us
    all_gather x1, waiting for transfers between devices, per_device(): lax.all_gather(w_up, 'dp', axis=1, tiled=True)  58.7 us
    all_to_all x1, waiting for transfers between devices, per_device(): lax.all_to_all(dy_slots, 'expert', split_axis=0, concat_axis=0, tiled=True)  24.1 us
    all_to_all x1, waiting for transfers between devices, per_device(): lax.all_to_all(x_grad.reshape(n_expert, capacity, model_width), 'expert',...  23 us
    all_to_all x1, waiting for transfers between devices, per_device(): lax.all_to_all(x_slots, 'expert', split_axis=0, concat_axis=0, tiled=True)  19.5 us
    reduce_scatter x1, waiting for transfers between devices, per_device(): lax.psum_scatter(lax.dot_general(scaled, hidden, (((0,), (0,)), ((), ()))...  17.8 us
    all_to_all x1, starting transfers between devices, per_device(): lax.all_to_all(p_slots, 'expert', split_axis=0, concat_axis=0, tiled=True)  9.43 us
    all_to_all x1, starting transfers between devices, per_device(): lax.all_to_all(dy_slots, 'expert', split_axis=0, concat_axis=0, tiled=True)  7.69 us
  transfers between devices with their start and end apart: 9, of which 7 were waited for; matrix products, arithmetic and copies ran while one was open for 19% of the time, Pallas kernels for 0%

commit v1 on v0

--- a/solution.py
+++ b/solution.py
@@ -2,6 +2,57 @@
 import jax.numpy as jnp
 from jax import lax
 from jax.sharding import PartitionSpec as P
+
+
+def ring_gather(shard, axis):
+    n = lax.axis_size(axis)
+    i = lax.axis_index(axis)
+    rows = shard.shape[1]
+    fwd = [(m, (m + 1) % n) for m in range(n)]
+    bwd = [(m, (m - 1) % n) for m in range(n)]
+    full = jnp.zeros((shard.shape[0], n * rows) + shard.shape[2:], shard.dtype)
+    full = lax.dynamic_update_slice_in_dim(full, shard, i * rows, axis=1)
+    f = shard
+    b = shard
+    for s in range(1, n // 2 + 1):
+        f = lax.ppermute(f, axis, fwd)
+        full = lax.dynamic_update_slice_in_dim(full, f, ((i - s) % n) * rows, axis=1)
+        if s <= (n - 1) // 2:
+            b = lax.ppermute(b, axis, bwd)
+            full = lax.dynamic_update_slice_in_dim(full, b, ((i + s) % n) * rows, axis=1)
+    return full
+
+
+def ring_reduce_scatter(partial, axis):
+    n = lax.axis_size(axis)
+    i = lax.axis_index(axis)
+    rows = partial.shape[0] // n
+    fwd = [(m, (m + 1) % n) for m in range(n)]
+    bwd = [(m, (m - 1) % n) for m in range(n)]
+
+    def chunk(k):
+        return lax.dynamic_slice_in_dim(partial, (k % n) * rows, rows, axis=0).astype(jnp.float32)
+
+    total = chunk(i)
+    nf = n // 2
+    nb = (n - 1) // 2
+    if nf > 0:
+        acc = chunk(i + nf).astype(partial.dtype)
+        for s in range(1, nf + 1):
+            got = lax.ppermute(acc, axis, fwd)
+            if s < nf:
+                acc = (got.astype(jnp.float32) + chunk(i + nf - s)).astype(partial.dtype)
+            else:
+                total = total + got.astype(jnp.float32)
+    if nb > 0:
+        acc = chunk(i - nb).astype(partial.dtype)
+        for s in range(1, nb + 1):
+            got = lax.ppermute(acc, axis, bwd)
+            if s < nb:
+                acc = (got.astype(jnp.float32) + chunk(i - nb + s)).astype(partial.dtype)
+            else:
+                total = total + got.astype(jnp.float32)
+    return total.astype(partial.dtype)
 
 
 def per_device(x_tokens, grad_out, expert_ids, route_probs, w_gate, w_up, w_down):
@@ -38,18 +89,15 @@
     dy_rows = arrived[1].reshape(slot_count, model_width)
     p_rows = arrived[2].reshape(slot_count).astype(jnp.float32)
     scaled = (p_rows[:, None] * dy_rows.astype(jnp.float32)).astype(jnp.bfloat16)
-    gate_full, up_full = (
-        lax.all_gather(w_gate, "dp", axis=1, tiled=True),
-        lax.all_gather(w_up, "dp", axis=1, tiled=True),
-    )
-    gate_full = gate_full[0]
-    up_full = up_full[0]
+    full = ring_gather(jnp.stack([w_gate[0], w_up[0], w_down[0]]), "dp")
+    gate_full = full[0]
+    up_full = full[1]
     gate_pre = jnp.dot(in_rows, gate_full, preferred_element_type=jnp.float32)
     up_pre = jnp.dot(in_rows, up_full, preferred_element_type=jnp.float32)
     gate_sig = jax.nn.sigmoid(gate_pre)
     gate_act = gate_pre * gate_sig
     hidden = (gate_act * up_pre).astype(jnp.bfloat16)
-    piece_rows = lax.all_gather(w_down, "dp", axis=1, tiled=True)[0]
+    piece_rows = full[2]
     out_piece = jnp.dot(hidden, piece_rows.T, preferred_element_type=jnp.float32)
     grad_sum = jnp.dot(scaled, piece_rows, preferred_element_type=jnp.float32)
     prob_sum = jnp.sum(dy_rows.astype(jnp.float32) * out_piece, axis=1)
@@ -62,13 +110,11 @@
         jnp.dot(gate_grad, gate_full.T, preferred_element_type=jnp.float32)
         + jnp.dot(up_grad, up_full.T, preferred_element_type=jnp.float32)
     ).astype(jnp.bfloat16)
-    down_grad = lax.psum_scatter(
+    down_grad = ring_reduce_scatter(
         lax.dot_general(
             scaled, hidden, (((0,), (0,)), ((), ())), preferred_element_type=jnp.float32
         ).astype(jnp.bfloat16),
         "dp",
-        scatter_dimension=0,
-        tiled=True,
     )
     grad_w_down = down_grad[None]
     returned = (

time: 323 us -> 312 us (0.966)
  the two profiles are of different devices: /device:TPU:4 before, /device:TPU:1 now
where the time goes in v1:
time: 312 us; the launch traced here: 309 us
  starting transfers between devices  150 us (48%)
  local copies, waits for them, and re-layouts  65.9 us (21%)
  waiting for transfers between devices  49.4 us (16%)
  matrix products  26.8 us (9%)
  other arithmetic  14.8 us (5%)
    ppermute x7, starting transfers between devices, ring_gather(): b = lax.ppermute(b, axis, bwd)  38.8 us
    ppermute x7, starting transfers between devices, ring_reduce_scatter(): got = lax.ppermute(acc, axis, bwd)  34.2 us
    ppermute x7, waiting for transfers between devices, ring_gather(): b = lax.ppermute(b, axis, bwd)  20.2 us
    ppermute x8, starting transfers between devices, ring_gather(): f = lax.ppermute(f, axis, fwd)  17.9 us
    ppermute x8, waiting for transfers between devices, ring_gather(): f = lax.ppermute(f, axis, fwd)  17.9 us
    ppermute x8, starting transfers between devices, ring_reduce_scatter(): got = lax.ppermute(acc, axis, fwd)  15.5 us
    all_to_all x1, starting transfers between devices, per_device(): lax.all_to_all(prob_sum.astype(jnp.bfloat16).reshape(n_expert, capacity),...  13.1 us
    dynamic_update_slice x8, local copies, waits for them, and re-layouts, ring_gather(): full = lax.dynamic_update_slice_in_dim(full, f, (i - s) % n * rows, axis=1)  12.3 us
  transfers between devices with their start and end apart: 35, of which 13 were waited for; matrix products, arithmetic and copies ran while one was open for 29% of the time, Pallas kernels for 0%

profile of v1, /device:TPU:1, one launch (start us, length us, event | category | flops | bytes accessed | tf_op | source)
XLA Modules:
  0.0 308.9 jit_solution(6519168075634244982)
XLA Ops:
  3.5 4.4 %collective-permute-start = (bf16[3,128,768]{2,1,0:T(8,128)(2,1)S(1)}, bf16[3,128,768]{2,1,0:T(8,128)(2,1)S(1)}, u32[]{:S(2)}, u32[]{:S(2)}) collective-permute-start(bf16[3,128,768]{2,1,0:T(8,128)(2,1)S(1)} %constant_dynamic-update-slice_fusion.16), channel_id=1, source_target_pairs={{0,32},{32,64},{64,96},{96,128},{128,160},{160,192},{192,224},{224... | collective-permute-start | bytes 1769480 | tf_op jit(solution)/shard_map/ppermute | solution.py:18
  7.9 9.5 %collective-permute-start.1 = (bf16[3,128,768]{2,1,0:T(8,128)(2,1)S(1)}, bf16[3,128,768]{2,1,0:T(8,128)(2,1)}, u32[]{:S(2)}, u32[]{:S(2)}) collective-permute-start(bf16[3,128,768]{2,1,0:T(8,128)(2,1)S(1)} %constant_dynamic-update-slice_fusion.16), channel_id=1, source_target_pairs={{0,480},{32,0},{64,32},{96,64},{128,96},{160,128},{192,160},{224,1... | collective-permute-start | bytes 1769480 | tf_op jit(solution)/shard_map/ppermute | solution.py:21
  22.8 5.7 %collective-permute-done = bf16[3,128,768]{2,1,0:T(8,128)(2,1)S(1)} collective-permute-done((bf16[3,128,768]{2,1,0:T(8,128)(2,1)S(1)}, bf16[3,128,768]{2,1,0:T(8,128)(2,1)S(1)}, u32[]{:S(2)}, u32[]{:S(2)}) %collective-permute-start) | collective-permute-done | bytes 589856 | tf_op jit(solution)/shard_map/ppermute | solution.py:18
  30.5 2.5 gather_fusion
  33.7 8.3 %all-to-all-start = ((bf16[32,1,10]{2,1,0:T(2,128)(2,1)}), bf16[32,1,10]{2,1,0:T(2,128)(2,1)S(1)}, u32[]{:S(2)}, u32[]{:S(2)}) async-start(bf16[32,1,10]{2,1,0:T(2,128)(2,1)} %all_to_all.25), calls=%async_computation | async-start | bytes 32768 | tf_op jit(solution)/shard_map/all_to_all | solution.py:86
  42.1 2.4 gather_fusion.2
  46.1 2.8 all-to-all-done
  48.9 5.0 %all-to-all-start.2 = ((bf16[32,10,2048]{2,1,0:T(8,128)(2,1)}), bf16[32,10,2048]{2,1,0:T(8,128)(2,1)}, u32[]{:S(2)}, u32[]{:S(2)}) async-start(bf16[32,10,2048]{2,1,0:T(8,128)(2,1)} %reshape.123), calls=%async_computation.2 | async-start | bytes 4194304 | tf_op jit(solution)/shard_map/all_to_all | solution.py:84
  53.9 4.9 %collective-permute-start.3 = (bf16[3,128,768]{2,1,0:T(8,128)(2,1)}, bf16[3,128,768]{2,1,0:T(8,128)(2,1)S(1)}, u32[]{:S(2)}, u32[]{:S(2)}) collective-permute-start(bf16[3,128,768]{2,1,0:T(8,128)(2,1)} %collective-permute-done.1), channel_id=1, source_target_pairs={{0,480},{32,0},{64,32},{96,64},{128,96},{160,128},{192,160},{224,1... | collective-permute-start | bytes 1769480 | tf_op jit(solution)/shard_map/ppermute | solution.py:21
  60.7 10.6 %collective-permute-done.3 = bf16[3,128,768]{2,1,0:T(8,128)(2,1)S(1)} collective-permute-done((bf16[3,128,768]{2,1,0:T(8,128)(2,1)}, bf16[3,128,768]{2,1,0:T(8,128)(2,1)S(1)}, u32[]{:S(2)}, u32[]{:S(2)}) %collective-permute-start.3) | collective-permute-done | bytes 589856 | tf_op jit(solution)/shard_map/ppermute | solution.py:21
  71.3 5.3 %collective-permute-start.5 = (bf16[3,128,768]{2,1,0:T(8,128)(2,1)S(1)}, bf16[3,128,768]{2,1,0:T(8,128)(2,1)}, u32[]{:S(2)}, u32[]{:S(2)}) collective-permute-start(bf16[3,128,768]{2,1,0:T(8,128)(2,1)S(1)} %collective-permute-done.3), channel_id=1, source_target_pairs={{0,480},{32,0},{64,32},{96,64},{128,96},{160,128},{192,160},{224,1... | collective-permute-start | bytes 1769480 | tf_op jit(solution)/shard_map/ppermute | solution.py:21
  78.6 9.6 %collective-permute-done.5 = bf16[3,128,768]{2,1,0:T(8,128)(2,1)} collective-permute-done((bf16[3,128,768]{2,1,0:T(8,128)(2,1)S(1)}, bf16[3,128,768]{2,1,0:T(8,128)(2,1)}, u32[]{:S(2)}, u32[]{:S(2)}) %collective-permute-start.5) | collective-permute-done | bytes 589856 | tf_op jit(solution)/shard_map/ppermute | solution.py:21
  88.2 5.4 %collective-permute-start.7 = (bf16[3,128,768]{2,1,0:T(8,128)(2,1)}, bf16[3,128,768]{2,1,0:T(8,128)(2,1)}, u32[]{:S(2)}, u32[]{:S(2)}) collective-permute-start(bf16[3,128,768]{2,1,0:T(8,128)(2,1)} %collective-permute-done.5), channel_id=1, source_target_pairs={{0,480},{32,0},{64,32},{96,64},{128,96},{160,128},{192,160},{224,1... | collective-permute-start | bytes 1769480 | tf_op jit(solution)/shard_map/ppermute | solution.py:21
  93.6 2.4 gather_fusion.1
  97.6 9.4 %all-to-all-start.1 = ((bf16[32,10,2048]{2,1,0:T(8,128)(2,1)}), bf16[32,10,2048]{2,1,0:T(8,128)(2,1)S(1)}, u32[]{:S(2)}, u32[]{:S(2)}) async-start(bf16[32,10,2048]{2,1,0:T(8,128)(2,1)} %reshape.122), calls=%async_computation.1 | async-start | bytes 4194304 | tf_op jit(solution)/shard_map/all_to_all | solution.py:85
  109.3 4.6 %collective-permute-start.9 = (bf16[3,128,768]{2,1,0:T(8,128)(2,1)}, bf16[3,128,768]{2,1,0:T(8,128)(2,1)}, u32[]{:S(2)}, u32[]{:S(2)}) collective-permute-start(bf16[3,128,768]{2,1,0:T(8,128)(2,1)} %collective-permute-done.7), channel_id=1, source_target_pairs={{0,480},{32,0},{64,32},{96,64},{128,96},{160,128},{192,160},{224,1... | collective-permute-start | bytes 1769480 | tf_op jit(solution)/shard_map/ppermute | solution.py:21
  113.9 4.3 %broadcast_in_dim.25 = bf16[3,2048,768]{2,1,0:T(8,128)(2,1)} broadcast(bf16[]{:T(256)} %constant.205.clone.1), dimensions={} | broadcast | bytes 9437186 | tf_op jit(solution)/shard_map/broadcast_in_dim | solution.py:13
  119.1 6.1 %collective-permute-done.8 = bf16[3,128,768]{2,1,0:T(8,128)(2,1)} collective-permute-done((bf16[3,128,768]{2,1,0:T(8,128)(2,1)}, bf16[3,128,768]{2,1,0:T(8,128)(2,1)}, u32[]{:S(2)}, u32[]{:S(2)}) %collective-permute-start.8) | collective-permute-done | bytes 589856 | tf_op jit(solution)/shard_map/ppermute | solution.py:18
  132.0 4.6 %collective-permute-start.11 = (bf16[3,128,768]{2,1,0:T(8,128)(2,1)}, bf16[3,128,768]{2,1,0:T(8,128)(2,1)}, u32[]{:S(2)}, u32[]{:S(2)}) collective-permute-start(bf16[3,128,768]{2,1,0:T(8,128)(2,1)} %collective-permute-done.9), channel_id=1, source_target_pairs={{0,480},{32,0},{64,32},{96,64},{128,96},{160,128},{192,160},{224,1... | collective-permute-start | bytes 1769480 | tf_op jit(solution)/shard_map/ppermute | solution.py:21
  137.5 2.5 reshape.124
  152.0 4.6 %collective-permute-start.13 = (bf16[3,128,768]{2,1,0:T(8,128)(2,1)}, bf16[3,128,768]{2,1,0:T(8,128)(2,1)S(1)}, u32[]{:S(2)}, u32[]{:S(2)}) collective-permute-start(bf16[3,128,768]{2,1,0:T(8,128)(2,1)} %collective-permute-done.11), channel_id=1, source_target_pairs={{0,480},{32,0},{64,32},{96,64},{128,96},{160,128},{192,160},{224,1... | collective-permute-start | bytes 1769480 | tf_op jit(solution)/shard_map/ppermute | solution.py:21
  158.6 2.1 collective-permute-start.14
  160.7 2.0 constant_dynamic-update-slice_fusion.5
  164.6 2.0 constant_dynamic-update-slice_fusion.3
  168.4 5.4 %collective-permute-done.14 = bf16[3,128,768]{2,1,0:T(8,128)(2,1)S(1)} collective-permute-done((bf16[3,128,768]{2,1,0:T(8,128)(2,1)S(1)}, bf16[3,128,768]{2,1,0:T(8,128)(2,1)S(1)}, u32[]{:S(2)}, u32[]{:S(2)}) %collective-permute-start.14) | collective-permute-done | bytes 589856 | tf_op jit(solution)/shard_map/ppermute | solution.py:18
  174.7 3.1 fusion.3
  177.8 4.4 %multiply_convert_fusion.3 = (bf16[320,768]{1,0:T(8,128)(2,1)S(1)}, f32[320,768]{1,0:T(8,128)}) fusion(f32[320,768]{1,0:T(8,128)S(1)} %fusion.3, bf16[320,2048]{1,0:T(8,128)(2,1)S(1)} %reshape.124, bf16[3,2048,768]{2,1,0:T(8,128)(2,1)} %constant_dynamic-update-slice_fusion), kind=kOutput, calls=%fused_computation.21 | convolution fusion | flops 1008107520 | bytes 6914048 | tf_op jit(solution)/shard_map/dot_general | solution.py:96
  182.2 2.0 convolution_convert_fusion
  188.0 3.6 %convert_element_type.213 = bf16[320,2048]{1,0:T(8,128)(2,1)} reshape(bf16[32,10,2048]{2,1,0:T(8,128)(2,1)} %multiply_convert_fusion) | data formatting | bytes 2621440 | tf_op jit(solution)/shard_map/convert_element_type | solution.py:91
  191.5 4.6 %collective-permute-start.23 = (bf16[128,768]{1,0:T(8,128)(2,1)S(1)}, bf16[128,768]{1,0:T(8,128)(2,1)S(1)}, u32[]{:S(2)}, u32[]{:S(2)}) collective-permute-start(bf16[128,768]{1,0:T(8,128)(2,1)S(1)} %get-tuple-element.22), channel_id=1, source_target_pairs={{0,480},{32,0},{64,32},{96,64},{128,96},{160,128},{192,160},{224,1... | collective-permute-start | bytes 589832 | tf_op jit(solution)/shard_map/ppermute | solution.py:50
  197.1 2.1 collective-permute-start.16
  199.2 3.5 %fusion = f32[320,768]{1,0:T(8,128)S(1)} fusion(bf16[320,2048]{1,0:T(8,128)(2,1)} %convert_element_type.213, bf16[3,2048,768]{2,1,0:T(8,128)(2,1)} %constant_dynamic-update-slice_fusion), kind=kOutput, calls=%fused_computation.13 | convolution fusion | flops 1006632960 | bytes 5439488 | tf_op jit(solution)/shard_map/dot_general | solution.py:102
  202.6 2.2 collective-permute-done.16
  206.9 4.8 %collective-permute-start.24 = (bf16[128,768]{1,0:T(8,128)(2,1)S(1)}, bf16[128,768]{1,0:T(8,128)(2,1)S(1)}, u32[]{:S(2)}, u32[]{:S(2)}) collective-permute-start(bf16[128,768]{1,0:T(8,128)(2,1)S(1)} %get-tuple-element.20), channel_id=1, source_target_pairs={{0,480},{32,0},{64,32},{96,64},{128,96},{160,128},{192,160},{224,1... | collective-permute-start | bytes 589832 | tf_op jit(solution)/shard_map/ppermute | solution.py:50
  211.8 4.6 %fusion.1 = f32[320,2048]{1,0:T(8,128)} fusion(bf16[3,2048,768]{2,1,0:T(8,128)(2,1)} %constant_dynamic-update-slice_fusion, f32[320,768]{1,0:T(8,128)S(1)} %fusion, f32[320,768]{1,0:T(8,128)S(1)} %copy-done.13), kind=kOutput, calls=%fused_computation.14 | convolution fusion | flops 1008107520 | bytes 7733248 | tf_op jit(solution)/shard_map/dot_general | solution.py:111
  219.1 4.6 %collective-permute-start.25 = (bf16[128,768]{1,0:T(8,128)(2,1)S(1)}, bf16[128,768]{1,0:T(8,128)(2,1)}, u32[]{:S(2)}, u32[]{:S(2)}) collective-permute-start(bf16[128,768]{1,0:T(8,128)(2,1)S(1)} %get-tuple-element.18), channel_id=1, source_target_pairs={{0,480},{32,0},{64,32},{96,64},{128,96},{160,128},{192,160},{224,1... | collective-permute-start | bytes 589832 | tf_op jit(solution)/shard_map/ppermute | solution.py:50
  223.7 3.3 %fusion.5 = bf16[320]{0:T(512)(128)(2,1)S(1)} fusion(f32[320,2048]{1,0:T(8,128)S(1)} %copy-done.2, bf16[320,768]{1,0:T(8,128)(2,1)S(1)} %copy-done.10, bf16[3,2048,768]{2,1,0:T(8,128)(2,1)} %constant_dynamic-update-slice_fusion), kind=kOutput, calls=%fused_computation.19 | convolution fusion | flops 1007943360 | bytes 6259328 | tf_op jit(solution)/shard_map/dot_general | solution.py:101
  227.7 13.1 %all-to-all-start.4 = ((bf16[32,1,10]{2,1,0:T(2,128)(2,1)}), bf16[32,1,10]{2,1,0:T(2,128)(2,1)S(1)}, u32[]{:S(2)}, u32[]{:S(2)}) async-start(bf16[32,1,10]{2,1,0:T(2,128)(2,1)} %convert_element_type.272), calls=%async_computation.4 | async-start | bytes 32768 | tf_op jit(solution)/shard_map/all_to_all | solution.py:128
  244.5 4.6 %collective-permute-start.26 = (bf16[128,768]{1,0:T(8,128)(2,1)S(1)}, bf16[128,768]{1,0:T(8,128)(2,1)}, u32[]{:S(2)}, u32[]{:S(2)}) collective-permute-start(bf16[128,768]{1,0:T(8,128)(2,1)S(1)} %get-tuple-element.16), channel_id=1, source_target_pairs={{0,480},{32,0},{64,32},{96,64},{128,96},{160,128},{192,160},{224,1... | collective-permute-start | bytes 589832 | tf_op jit(solution)/shard_map/ppermute | solution.py:50
  249.0 6.0 %fusion.4 = bf16[320,2048]{1,0:T(8,128)(2,1)} fusion(f32[320,2048]{1,0:T(8,128)} %fusion.1, bf16[3,2048,768]{2,1,0:T(8,128)(2,1)} %constant_dynamic-update-slice_fusion, f32[320,768]{1,0:T(8,128)} %copy-done.12, f32[320,768]{1,0:T(8,128)} %copy-done.14, f32[320,768]{1,0:T(8,128)} %get-tuple-element.26), kind=kOutput, calls=%fused_computation.17 | convolution fusion | flops 1010401280 | bytes 10027008 | tf_op jit(solution)/shard_map/dot_general | solution.py:110
  255.0 3.4 %reshape.125 = bf16[32,10,2048]{2,1,0:T(8,128)(2,1)} reshape(bf16[320,2048]{1,0:T(8,128)(2,1)} %fusion.4) | data formatting | bytes 2621440 | tf_op jit(solution)/shard_map/reshape | solution.py:122
  258.4 8.0 %all-to-all-start.3 = ((bf16[32,10,2048]{2,1,0:T(8,128)(2,1)}), bf16[32,10,2048]{2,1,0:T(8,128)(2,1)}, u32[]{:S(2)}, u32[]{:S(2)}) async-start(bf16[32,10,2048]{2,1,0:T(8,128)(2,1)} %reshape.125), calls=%async_computation.3 | async-start | bytes 4194304 | tf_op jit(solution)/shard_map/all_to_all | solution.py:121
  269.4 4.6 %collective-permute-start.27 = (bf16[128,768]{1,0:T(8,128)(2,1)S(1)}, bf16[128,768]{1,0:T(8,128)(2,1)S(1)}, u32[]{:S(2)}, u32[]{:S(2)}) collective-permute-start(bf16[128,768]{1,0:T(8,128)(2,1)S(1)} %get-tuple-element.14), channel_id=1, source_target_pairs={{0,480},{32,0},{64,32},{96,64},{128,96},{160,128},{192,160},{224,1... | collective-permute-start | bytes 589832 | tf_op jit(solution)/shard_map/ppermute | solution.py:50
  273.9 2.8 collective-permute-done.20
  279.6 5.6 %collective-permute-start.28 = (bf16[128,768]{1,0:T(8,128)(2,1)S(1)}, bf16[128,768]{1,0:T(8,128)(2,1)S(1)}, u32[]{:S(2)}, u32[]{:S(2)}) collective-permute-start(bf16[128,768]{1,0:T(8,128)(2,1)S(1)} %get-tuple-element.12), channel_id=1, source_target_pairs={{0,480},{32,0},{64,32},{96,64},{128,96},{160,128},{192,160},{224,1... | collective-permute-start | bytes 589832 | tf_op jit(solution)/shard_map/ppermute | solution.py:50
  288.1 5.4 %collective-permute-start.29 = (bf16[128,768]{1,0:T(8,128)(2,1)S(1)}, bf16[128,768]{1,0:T(8,128)(2,1)S(1)}, u32[]{:S(2)}, u32[]{:S(2)}) collective-permute-start(bf16[128,768]{1,0:T(8,128)(2,1)S(1)} %get-tuple-element.10), channel_id=1, source_target_pairs={{0,480},{32,0},{64,32},{96,64},{128,96},{160,128},{192,160},{224,1... | collective-permute-start | bytes 589832 | tf_op jit(solution)/shard_map/ppermute | solution.py:50
  299.0 2.5 reshape.126
  303.6 3.6 %reduce_sum.34 = bf16[128,2048]{1,0:T(8,128)(2,1)} reduce(bf16[128,2,2048]{2,1,0:T(2,128)(2,1)S(1)} %gather.21, bf16[]{:T(256)} %constant.205.clone.1), dimensions={1}, to_apply=%region_4.5 | reduce | flops 262144 | bytes 1572866 | tf_op jit(solution)/shard_map/reduce_sum | solution.py:139
  (136 shorter events, 78.6 us)
Async XLA Ops:
  0.6 41.4 %copy-start.7 = (bf16[128,2048]{1,0:T(8,128)(2,1)S(1)}, bf16[128,2048]{1,0:T(8,128)(2,1)}, u32[]{:S(2)}) copy-start(bf16[128,2048]{1,0:T(8,128)(2,1)} %param.7) | copy-start | bytes 1572868
  3.5 25.0 %collective-permute-start = (bf16[3,128,768]{2,1,0:T(8,128)(2,1)S(1)}, bf16[3,128,768]{2,1,0:T(8,128)(2,1)S(1)}, u32[]{:S(2)}, u32[]{:S(2)}) collective-permute-start(bf16[3,128,768]{2,1,0:T(8,128)(2,1)S(1)} %constant_dynamic-update-slice_fusion.16), channel_id=1, source_target_pairs={{0,32},{32,64},{64,96},{96,128},{128,160},{160,192},{192,224},{224... | collective-permute-start | bytes 1769480 | tf_op jit(solution)/shard_map/ppermute | solution.py:18
  7.9 46.0 %collective-permute-start.1 = (bf16[3,128,768]{2,1,0:T(8,128)(2,1)S(1)}, bf16[3,128,768]{2,1,0:T(8,128)(2,1)}, u32[]{:S(2)}, u32[]{:S(2)}) collective-permute-start(bf16[3,128,768]{2,1,0:T(8,128)(2,1)S(1)} %constant_dynamic-update-slice_fusion.16), channel_id=1, source_target_pairs={{0,480},{32,0},{64,32},{96,64},{128,96},{160,128},{192,160},{224,1... | collective-permute-start | bytes 1769480 | tf_op jit(solution)/shard_map/ppermute | solution.py:21
  21.3 7.2 %copy-start.11 = (s32[256,1]{0,1:T(1,128)}, s32[256,1]{0,1:T(1,128)S(1)}, u32[]{:S(2)}) copy-start(s32[256,1]{0,1:T(1,128)S(1)} %compare_select_fusion) | copy-start | bytes 3076
  28.5 30.3 %collective-permute-start.2 = (bf16[3,128,768]{2,1,0:T(8,128)(2,1)S(1)}, bf16[3,128,768]{2,1,0:T(8,128)(2,1)}, u32[]{:S(2)}, u32[]{:S(2)}) collective-permute-start(bf16[3,128,768]{2,1,0:T(8,128)(2,1)S(1)} %collective-permute-done), channel_id=1, source_target_pairs={{0,32},{32,64},{64,96},{96,128},{128,160},{160,192},{192,224},{224... | collective-permute-start | bytes 1769480 | tf_op jit(solution)/shard_map/ppermute | solution.py:18
  33.7 15.2 %all-to-all-start = ((bf16[32,1,10]{2,1,0:T(2,128)(2,1)}), bf16[32,1,10]{2,1,0:T(2,128)(2,1)S(1)}, u32[]{:S(2)}, u32[]{:S(2)}) async-start(bf16[32,1,10]{2,1,0:T(2,128)(2,1)} %all_to_all.25), calls=%async_computation | async-start | bytes 32768 | tf_op jit(solution)/shard_map/all_to_all | solution.py:86
  46.1 47.5 %copy-start.8 = (bf16[128,2048]{1,0:T(8,128)(2,1)S(1)}, bf16[128,2048]{1,0:T(8,128)(2,1)}, u32[]{:S(2)}) copy-start(bf16[128,2048]{1,0:T(8,128)(2,1)} %param.8) | copy-start | bytes 1572868
  48.9 48.7 %all-to-all-start.2 = ((bf16[32,10,2048]{2,1,0:T(8,128)(2,1)}), bf16[32,10,2048]{2,1,0:T(8,128)(2,1)}, u32[]{:S(2)}, u32[]{:S(2)}) async-start(bf16[32,10,2048]{2,1,0:T(8,128)(2,1)} %reshape.123), calls=%async_computation.2 | async-start | bytes 4194304 | tf_op jit(solution)/shard_map/all_to_all | solution.py:84
  53.9 17.4 %collective-permute-start.3 = (bf16[3,128,768]{2,1,0:T(8,128)(2,1)}, bf16[3,128,768]{2,1,0:T(8,128)(2,1)S(1)}, u32[]{:S(2)}, u32[]{:S(2)}) collective-permute-start(bf16[3,128,768]{2,1,0:T(8,128)(2,1)} %collective-permute-done.1), channel_id=1, source_target_pairs={{0,480},{32,0},{64,32},{96,64},{128,96},{160,128},{192,160},{224,1... | collective-permute-start | bytes 1769480 | tf_op jit(solution)/shard_map/ppermute | solution.py:21
  58.8 17.9 %collective-permute-start.4 = (bf16[3,128,768]{2,1,0:T(8,128)(2,1)}, bf16[3,128,768]{2,1,0:T(8,128)(2,1)}, u32[]{:S(2)}, u32[]{:S(2)}) collective-permute-start(bf16[3,128,768]{2,1,0:T(8,128)(2,1)} %collective-permute-done.2), channel_id=1, source_target_pairs={{0,32},{32,64},{64,96},{96,128},{128,160},{160,192},{192,224},{224... | collective-permute-start | bytes 1769480 | tf_op jit(solution)/shard_map/ppermute | solution.py:18
  71.3 16.8 %copy-start.5 = (bf16[3,128,768]{2,1,0:T(8,128)(2,1)}, bf16[3,128,768]{2,1,0:T(8,128)(2,1)S(1)}, u32[]{:S(2)}) copy-start(bf16[3,128,768]{2,1,0:T(8,128)(2,1)S(1)} %collective-permute-done.3) | copy-start | bytes 1769476
  71.3 16.8 %collective-permute-start.5 = (bf16[3,128,768]{2,1,0:T(8,128)(2,1)S(1)}, bf16[3,128,768]{2,1,0:T(8,128)(2,1)}, u32[]{:S(2)}, u32[]{:S(2)}) collective-permute-start(bf16[3,128,768]{2,1,0:T(8,128)(2,1)S(1)} %collective-permute-done.3), channel_id=1, source_target_pairs={{0,480},{32,0},{64,32},{96,64},{128,96},{160,128},{192,160},{224,1... | collective-permute-start | bytes 1769480 | tf_op jit(solution)/shard_map/ppermute | solution.py:21
  76.7 30.4 %collective-permute-start.6 = (bf16[3,128,768]{2,1,0:T(8,128)(2,1)}, bf16[3,128,768]{2,1,0:T(8,128)(2,1)}, u32[]{:S(2)}, u32[]{:S(2)}) collective-permute-start(bf16[3,128,768]{2,1,0:T(8,128)(2,1)} %collective-permute-done.4), channel_id=1, source_target_pairs={{0,32},{32,64},{64,96},{96,128},{128,160},{160,192},{192,224},{224... | collective-permute-start | bytes 1769480 | tf_op jit(solution)/shard_map/ppermute | solution.py:18
  88.2 21.2 %collective-permute-start.7 = (bf16[3,128,768]{2,1,0:T(8,128)(2,1)}, bf16[3,128,768]{2,1,0:T(8,128)(2,1)}, u32[]{:S(2)}, u32[]{:S(2)}) collective-permute-start(bf16[3,128,768]{2,1,0:T(8,128)(2,1)} %collective-permute-done.5), channel_id=1, source_target_pairs={{0,480},{32,0},{64,32},{96,64},{128,96},{160,128},{192,160},{224,1... | collective-permute-start | bytes 1769480 | tf_op jit(solution)/shard_map/ppermute | solution.py:21
  97.6 42.4 %all-to-all-start.1 = ((bf16[32,10,2048]{2,1,0:T(8,128)(2,1)}), bf16[32,10,2048]{2,1,0:T(8,128)(2,1)S(1)}, u32[]{:S(2)}, u32[]{:S(2)}) async-start(bf16[32,10,2048]{2,1,0:T(8,128)(2,1)} %reshape.122), calls=%async_computation.1 | async-start | bytes 4194304 | tf_op jit(solution)/shard_map/all_to_all | solution.py:85
  107.1 18.1 %collective-permute-start.8 = (bf16[3,128,768]{2,1,0:T(8,128)(2,1)}, bf16[3,128,768]{2,1,0:T(8,128)(2,1)}, u32[]{:S(2)}, u32[]{:S(2)}) collective-permute-start(bf16[3,128,768]{2,1,0:T(8,128)(2,1)} %collective-permute-done.6), channel_id=1, source_target_pairs={{0,32},{32,64},{64,96},{96,128},{128,160},{160,192},{192,224},{224... | collective-permute-start | bytes 1769480 | tf_op jit(solution)/shard_map/ppermute | solution.py:18
  109.3 22.7 %collective-permute-start.9 = (bf16[3,128,768]{2,1,0:T(8,128)(2,1)}, bf16[3,128,768]{2,1,0:T(8,128)(2,1)}, u32[]{:S(2)}, u32[]{:S(2)}) collective-permute-start(bf16[3,128,768]{2,1,0:T(8,128)(2,1)} %collective-permute-done.7), channel_id=1, source_target_pairs={{0,480},{32,0},{64,32},{96,64},{128,96},{160,128},{192,160},{224,1... | collective-permute-start | bytes 1769480 | tf_op jit(solution)/shard_map/ppermute | solution.py:21
  119.1 17.6 %copy-start.6 = (bf16[3,128,768]{2,1,0:T(8,128)(2,1)S(1)}, bf16[3,128,768]{2,1,0:T(8,128)(2,1)}, u32[]{:S(2)}) copy-start(bf16[3,128,768]{2,1,0:T(8,128)(2,1)} %copy-done.5) | copy-start | bytes 1769476
  125.2 17.2 %collective-permute-start.10 = (bf16[3,128,768]{2,1,0:T(8,128)(2,1)}, bf16[3,128,768]{2,1,0:T(8,128)(2,1)}, u32[]{:S(2)}, u32[]{:S(2)}) collective-permute-start(bf16[3,128,768]{2,1,0:T(8,128)(2,1)} %collective-permute-done.8), channel_id=1, source_target_pairs={{0,32},{32,64},{64,96},{96,128},{128,160},{160,192},{192,224},{224... | collective-permute-start | bytes 1769480 | tf_op jit(solution)/shard_map/ppermute | solution.py:18
  132.0 20.0 %collective-permute-start.11 = (bf16[3,128,768]{2,1,0:T(8,128)(2,1)}, bf16[3,128,768]{2,1,0:T(8,128)(2,1)}, u32[]{:S(2)}, u32[]{:S(2)}) collective-permute-start(bf16[3,128,768]{2,1,0:T(8,128)(2,1)} %collective-permute-done.9), channel_id=1, source_target_pairs={{0,480},{32,0},{64,32},{96,64},{128,96},{160,128},{192,160},{224,1... | collective-permute-start | bytes 1769480 | tf_op jit(solution)/shard_map/ppermute | solution.py:21
  140.0 8.2 %copy-start.3 = (bf16[32,10,2048]{2,1,0:T(8,128)(2,1)}, bf16[32,10,2048]{2,1,0:T(8,128)(2,1)S(1)}, u32[]{:S(2)}) copy-start(bf16[32,10,2048]{2,1,0:T(8,128)(2,1)S(1)} %all-to-all-done.1) | copy-start | bytes 3932164
  142.4 16.2 %collective-permute-start.12 = (bf16[3,128,768]{2,1,0:T(8,128)(2,1)}, bf16[3,128,768]{2,1,0:T(8,128)(2,1)S(1)}, u32[]{:S(2)}, u32[]{:S(2)}) collective-permute-start(bf16[3,128,768]{2,1,0:T(8,128)(2,1)} %collective-permute-done.10), channel_id=1, source_target_pairs={{0,32},{32,64},{64,96},{96,128},{128,160},{160,192},{192,224},{224... | collective-permute-start | bytes 1769480 | tf_op jit(solution)/shard_map/ppermute | solution.py:18
  152.0 15.5 %collective-permute-start.13 = (bf16[3,128,768]{2,1,0:T(8,128)(2,1)}, bf16[3,128,768]{2,1,0:T(8,128)(2,1)S(1)}, u32[]{:S(2)}, u32[]{:S(2)}) collective-permute-start(bf16[3,128,768]{2,1,0:T(8,128)(2,1)} %collective-permute-done.11), channel_id=1, source_target_pairs={{0,480},{32,0},{64,32},{96,64},{128,96},{160,128},{192,160},{224,1... | collective-permute-start | bytes 1769480 | tf_op jit(solution)/shard_map/ppermute | solution.py:21
  158.6 15.2 %collective-permute-start.14 = (bf16[3,128,768]{2,1,0:T(8,128)(2,1)S(1)}, bf16[3,128,768]{2,1,0:T(8,128)(2,1)S(1)}, u32[]{:S(2)}, u32[]{:S(2)}) collective-permute-start(bf16[3,128,768]{2,1,0:T(8,128)(2,1)S(1)} %collective-permute-done.12), channel_id=1, source_target_pairs={{0,32},{32,64},{64,96},{96,128},{128,160},{160,192},{192,224},{224... | collective-permute-start | bytes 1769480 | tf_op jit(solution)/shard_map/ppermute | solution.py:18
  177.8 4.5 %copy-start.12 = (f32[320,768]{1,0:T(8,128)}, f32[320,768]{1,0:T(8,128)S(1)}, u32[]{:S(2)}) copy-start(f32[320,768]{1,0:T(8,128)S(1)} %fusion.3) | copy-start | bytes 2949124
  177.8 4.5 %copy-start.1 = (f32[320,2048]{1,0:T(8,128)S(1)}, f32[320,2048]{1,0:T(8,128)}, u32[]{:S(2)}) copy-start(f32[320,2048]{1,0:T(8,128)} %reshape.130) | copy-start | bytes 7864324
  184.2 103.8 %copy-start = (bf16[2048,768]{1,0:T(8,128)(2,1)}, bf16[2048,768]{1,0:T(8,128)(2,1)S(1)}, u32[]{:S(2)}) copy-start(bf16[2048,768]{1,0:T(8,128)(2,1)S(1)} %convolution_convert_fusion) | copy-start | bytes 9437188
  184.2 11.8 %collective-permute-start.15 = (bf16[128,768]{1,0:T(8,128)(2,1)S(1)}, bf16[128,768]{1,0:T(8,128)(2,1)}, u32[]{:S(2)}, u32[]{:S(2)}) collective-permute-start(bf16[128,768]{1,0:T(8,128)(2,1)S(1)} %get-tuple-element.21), channel_id=1, source_target_pairs={{0,32},{32,64},{64,96},{96,128},{128,160},{160,192},{192,224},{224... | collective-permute-start | bytes 589832 | tf_op jit(solution)/shard_map/ppermute | solution.py:42
  191.5 11.1 %collective-permute-start.23 = (bf16[128,768]{1,0:T(8,128)(2,1)S(1)}, bf16[128,768]{1,0:T(8,128)(2,1)S(1)}, u32[]{:S(2)}, u32[]{:S(2)}) collective-permute-start(bf16[128,768]{1,0:T(8,128)(2,1)S(1)} %get-tuple-element.22), channel_id=1, source_target_pairs={{0,480},{32,0},{64,32},{96,64},{128,96},{160,128},{192,160},{224,1... | collective-permute-start | bytes 589832 | tf_op jit(solution)/shard_map/ppermute | solution.py:50
  197.1 14.7 %copy-start.13 = (f32[320,768]{1,0:T(8,128)S(1)}, f32[320,768]{1,0:T(8,128)}, u32[]{:S(2)}) copy-start(f32[320,768]{1,0:T(8,128)} %copy-done.12) | copy-start | bytes 2949124
  197.1 7.8 %collective-permute-start.16 = (bf16[128,768]{1,0:T(8,128)(2,1)S(1)}, bf16[128,768]{1,0:T(8,128)(2,1)S(1)}, u32[]{:S(2)}, u32[]{:S(2)}) collective-permute-start(bf16[128,768]{1,0:T(8,128)(2,1)S(1)} %add_convert_fusion.13), channel_id=1, source_target_pairs={{0,32},{32,64},{64,96},{96,128},{128,160},{160,192},{192,224},{224... | collective-permute-start | bytes 589832 | tf_op jit(solution)/shard_map/ppermute | solution.py:42
  202.6 13.8 %copy-start.14 = (f32[320,768]{1,0:T(8,128)}, f32[320,768]{1,0:T(8,128)S(1)}, u32[]{:S(2)}) copy-start(f32[320,768]{1,0:T(8,128)S(1)} %fusion) | copy-start | bytes 2949124
  205.0 11.5 %collective-permute-start.17 = (bf16[128,768]{1,0:T(8,128)(2,1)S(1)}, bf16[128,768]{1,0:T(8,128)(2,1)S(1)}, u32[]{:S(2)}, u32[]{:S(2)}) collective-permute-start(bf16[128,768]{1,0:T(8,128)(2,1)S(1)} %get-tuple-element.19), channel_id=1, source_target_pairs={{0,32},{32,64},{64,96},{96,128},{128,160},{160,192},{192,224},{224... | collective-permute-start | bytes 589832 | tf_op jit(solution)/shard_map/ppermute | solution.py:42
  206.9 16.8 %copy-start.2 = (f32[320,2048]{1,0:T(8,128)S(1)}, f32[320,2048]{1,0:T(8,128)}, u32[]{:S(2)}) copy-start(f32[320,2048]{1,0:T(8,128)} %reshape.130) | copy-start | bytes 7864324
  206.9 16.8 %copy-start.10 = (bf16[320,768]{1,0:T(8,128)(2,1)S(1)}, bf16[320,768]{1,0:T(8,128)(2,1)}, u32[]{:S(2)}) copy-start(bf16[320,768]{1,0:T(8,128)(2,1)} %copy-done.9) | copy-start | bytes 1474564
  206.9 9.5 %collective-permute-start.24 = (bf16[128,768]{1,0:T(8,128)(2,1)S(1)}, bf16[128,768]{1,0:T(8,128)(2,1)S(1)}, u32[]{:S(2)}, u32[]{:S(2)}) collective-permute-start(bf16[128,768]{1,0:T(8,128)(2,1)S(1)} %get-tuple-element.20), channel_id=1, source_target_pairs={{0,480},{32,0},{64,32},{96,64},{128,96},{160,128},{192,160},{224,1... | collective-permute-start | bytes 589832 | tf_op jit(solution)/shard_map/ppermute | solution.py:50
  217.2 23.6 %collective-permute-start.18 = (bf16[128,768]{1,0:T(8,128)(2,1)}, bf16[128,768]{1,0:T(8,128)(2,1)S(1)}, u32[]{:S(2)}, u32[]{:S(2)}) collective-permute-start(bf16[128,768]{1,0:T(8,128)(2,1)} %get-tuple-element.17), channel_id=1, source_target_pairs={{0,32},{32,64},{64,96},{96,128},{128,160},{160,192},{192,224},{224... | collective-permute-start | bytes 589832 | tf_op jit(solution)/shard_map/ppermute | solution.py:42
  219.1 21.7 %collective-permute-start.25 = (bf16[128,768]{1,0:T(8,128)(2,1)S(1)}, bf16[128,768]{1,0:T(8,128)(2,1)}, u32[]{:S(2)}, u32[]{:S(2)}) collective-permute-start(bf16[128,768]{1,0:T(8,128)(2,1)S(1)} %get-tuple-element.18), channel_id=1, source_target_pairs={{0,480},{32,0},{64,32},{96,64},{128,96},{160,128},{192,160},{224,1... | collective-permute-start | bytes 589832 | tf_op jit(solution)/shard_map/ppermute | solution.py:50
  227.7 30.7 %all-to-all-start.4 = ((bf16[32,1,10]{2,1,0:T(2,128)(2,1)}), bf16[32,1,10]{2,1,0:T(2,128)(2,1)S(1)}, u32[]{:S(2)}, u32[]{:S(2)}) async-start(bf16[32,1,10]{2,1,0:T(2,128)(2,1)} %convert_element_type.272), calls=%async_computation.4 | async-start | bytes 32768 | tf_op jit(solution)/shard_map/all_to_all | solution.py:128
  242.5 23.8 %collective-permute-start.19 = (bf16[128,768]{1,0:T(8,128)(2,1)}, bf16[128,768]{1,0:T(8,128)(2,1)S(1)}, u32[]{:S(2)}, u32[]{:S(2)}) collective-permute-start(bf16[128,768]{1,0:T(8,128)(2,1)} %get-tuple-element.15), channel_id=1, source_target_pairs={{0,32},{32,64},{64,96},{96,128},{128,160},{160,192},{192,224},{224... | collective-permute-start | bytes 589832 | tf_op jit(solution)/shard_map/ppermute | solution.py:42
  244.5 21.9 %collective-permute-start.26 = (bf16[128,768]{1,0:T(8,128)(2,1)S(1)}, bf16[128,768]{1,0:T(8,128)(2,1)}, u32[]{:S(2)}, u32[]{:S(2)}) collective-permute-start(bf16[128,768]{1,0:T(8,128)(2,1)S(1)} %get-tuple-element.16), channel_id=1, source_target_pairs={{0,480},{32,0},{64,32},{96,64},{128,96},{160,128},{192,160},{224,1... | collective-permute-start | bytes 589832 | tf_op jit(solution)/shard_map/ppermute | solution.py:50
  258.4 40.6 %all-to-all-start.3 = ((bf16[32,10,2048]{2,1,0:T(8,128)(2,1)}), bf16[32,10,2048]{2,1,0:T(8,128)(2,1)}, u32[]{:S(2)}, u32[]{:S(2)}) async-start(bf16[32,10,2048]{2,1,0:T(8,128)(2,1)} %reshape.125), calls=%async_computation.3 | async-start | bytes 4194304 | tf_op jit(solution)/shard_map/all_to_all | solution.py:121
  267.4 9.4 %collective-permute-start.20 = (bf16[128,768]{1,0:T(8,128)(2,1)S(1)}, bf16[128,768]{1,0:T(8,128)(2,1)S(1)}, u32[]{:S(2)}, u32[]{:S(2)}) collective-permute-start(bf16[128,768]{1,0:T(8,128)(2,1)S(1)} %get-tuple-element.13), channel_id=1, source_target_pairs={{0,32},{32,64},{64,96},{96,128},{128,160},{160,192},{192,224},{224... | collective-permute-start | bytes 589832 | tf_op jit(solution)/shard_map/ppermute | solution.py:42
  269.4 8.2 %collective-permute-start.27 = (bf16[128,768]{1,0:T(8,128)(2,1)S(1)}, bf16[128,768]{1,0:T(8,128)(2,1)S(1)}, u32[]{:S(2)}, u32[]{:S(2)}) collective-permute-start(bf16[128,768]{1,0:T(8,128)(2,1)S(1)} %get-tuple-element.14), channel_id=1, source_target_pairs={{0,480},{32,0},{64,32},{96,64},{128,96},{160,128},{192,160},{224,1... | collective-permute-start | bytes 589832 | tf_op jit(solution)/shard_map/ppermute | solution.py:50
  277.7 9.5 %collective-permute-start.21 = (bf16[128,768]{1,0:T(8,128)(2,1)S(1)}, bf16[128,768]{1,0:T(8,128)(2,1)S(1)}, u32[]{:S(2)}, u32[]{:S(2)}) collective-permute-start(bf16[128,768]{1,0:T(8,128)(2,1)S(1)} %get-tuple-element.11), channel_id=1, source_target_pairs={{0,32},{32,64},{64,96},{96,128},{128,160},{160,192},{192,224},{224... | collective-permute-start | bytes 589832 | tf_op jit(solution)/shard_map/ppermute | solution.py:42
  279.6 8.3 %collective-permute-start.28 = (bf16[128,768]{1,0:T(8,128)(2,1)S(1)}, bf16[128,768]{1,0:T(8,128)(2,1)S(1)}, u32[]{:S(2)}, u32[]{:S(2)}) collective-permute-start(bf16[128,768]{1,0:T(8,128)(2,1)S(1)} %get-tuple-element.12), channel_id=1, source_target_pairs={{0,480},{32,0},{64,32},{96,64},{128,96},{160,128},{192,160},{224,1... | collective-permute-start | bytes 589832 | tf_op jit(solution)/shard_map/ppermute | solution.py:50
  288.1 19.1 %collective-permute-start.29 = (bf16[128,768]{1,0:T(8,128)(2,1)S(1)}, bf16[128,768]{1,0:T(8,128)(2,1)S(1)}, u32[]{:S(2)}, u32[]{:S(2)}) collective-permute-start(bf16[128,768]{1,0:T(8,128)(2,1)S(1)} %get-tuple-element.10), channel_id=1, source_target_pairs={{0,480},{32,0},{64,32},{96,64},{128,96},{160,128},{192,160},{224,1... | collective-permute-start | bytes 589832 | tf_op jit(solution)/shard_map/ppermute | solution.py:50
  293.5 13.7 %collective-permute-start.22 = (bf16[128,768]{1,0:T(8,128)(2,1)S(1)}, bf16[128,768]{1,0:T(8,128)(2,1)S(1)}, u32[]{:S(2)}, u32[]{:S(2)}) collective-permute-start(bf16[128,768]{1,0:T(8,128)(2,1)S(1)} %get-tuple-element.9), channel_id=1, source_target_pairs={{0,32},{32,64},{64,96},{96,128},{128,160},{160,192},{192,224},{224... | collective-permute-start | bytes 589832 | tf_op jit(solution)/shard_map/ppermute | solution.py:42
  (2 other events, 5.9 us)

commit v2 on v0

--- a/solution.py
+++ b/solution.py
@@ -2,6 +2,31 @@
 import jax.numpy as jnp
 from jax import lax
 from jax.sharding import PartitionSpec as P
+
+
+def ring_gather_rotated(shard, axis):
+    n = lax.axis_size(axis)
+    fwd = [(m, (m + 1) % n) for m in range(n)]
+    bwd = [(m, (m - 1) % n) for m in range(n)]
+    nf = n // 2
+    nb = (n - 1) // 2
+    f = shard
+    b = shard
+    got_f = {}
+    got_b = {}
+    for s in range(1, nf + 1):
+        f = lax.ppermute(f, axis, fwd)
+        got_f[s] = f
+        if s <= nb:
+            b = lax.ppermute(b, axis, bwd)
+            got_b[s] = b
+    pieces = [shard] + [got_b[k] for k in range(1, nb + 1)] + [got_f[n - k] for k in range(nb + 1, n)]
+    return jnp.concatenate(pieces, axis=1)
+
+
+def roll_cols(a, shift, width):
+    doubled = jnp.concatenate([a, a], axis=1)
+    return lax.dynamic_slice_in_dim(doubled, shift % width, width, axis=1)
 
 
 def per_device(x_tokens, grad_out, expert_ids, route_probs, w_gate, w_up, w_down):
@@ -38,14 +63,14 @@
     dy_rows = arrived[1].reshape(slot_count, model_width)
     p_rows = arrived[2].reshape(slot_count).astype(jnp.float32)
     scaled = (p_rows[:, None] * dy_rows.astype(jnp.float32)).astype(jnp.bfloat16)
-    gate_full, up_full = (
-        lax.all_gather(w_gate, "dp", axis=1, tiled=True),
-        lax.all_gather(w_up, "dp", axis=1, tiled=True),
-    )
-    gate_full = gate_full[0]
-    up_full = up_full[0]
-    gate_pre = jnp.dot(in_rows, gate_full, preferred_element_type=jnp.float32)
-    up_pre = jnp.dot(in_rows, up_full, preferred_element_type=jnp.float32)
+    dp_index = lax.axis_index("dp")
+    shard_rows = w_gate.shape[1]
+    gu_rot = ring_gather_rotated(jnp.stack([w_gate[0], w_up[0]]), "dp")
+    gate_full = gu_rot[0]
+    up_full = gu_rot[1]
+    in_rot = roll_cols(in_rows, dp_index * shard_rows, model_width)
+    gate_pre = jnp.dot(in_rot, gate_full, preferred_element_type=jnp.float32)
+    up_pre = jnp.dot(in_rot, up_full, preferred_element_type=jnp.float32)
     gate_sig = jax.nn.sigmoid(gate_pre)
     gate_act = gate_pre * gate_sig
     hidden = (gate_act * up_pre).astype(jnp.bfloat16)
@@ -58,10 +83,11 @@
     gate_grad = (hidden_grad * up_pre * gate_sig * (1.0 + gate_pre * (1.0 - gate_sig))).astype(
         jnp.bfloat16
     )
-    x_grad = (
+    x_grad_rot = (
         jnp.dot(gate_grad, gate_full.T, preferred_element_type=jnp.float32)
         + jnp.dot(up_grad, up_full.T, preferred_element_type=jnp.float32)
     ).astype(jnp.bfloat16)
+    x_grad = roll_cols(x_grad_rot, -dp_index * shard_rows, model_width)
     down_grad = lax.psum_scatter(
         lax.dot_general(
             scaled, hidden, (((0,), (0,)), ((), ())), preferred_element_type=jnp.float32

time: 323 us -> 283 us (0.88)
  the two profiles are of different devices: /device:TPU:4 before, /device:TPU:1 now
where the time goes in v2:
time: 283 us; the launch traced here: 278 us
  starting transfers between devices  97.7 us (35%)
  waiting for transfers between devices  78.4 us (28%)
  local copies, waits for them, and re-layouts  55.6 us (20%)
  matrix products  21.2 us (7%)
  between operations  14.7 us (5%)
  other arithmetic  9.95 us (4%)
    ppermute x7, starting transfers between devices, ring_gather_rotated(): b = lax.ppermute(b, axis, bwd)  39.1 us
    ppermute x7, waiting for transfers between devices, ring_gather_rotated(): b = lax.ppermute(b, axis, bwd)  33.1 us
    all_to_all x1, waiting for transfers between devices, per_device(): lax.all_to_all(x_grad.reshape(n_expert, capacity, model_width), 'expert',...  25.4 us
    unnamed x51, local copies, waits for them, and re-layouts  22.4 us
    ppermute x8, starting transfers between devices, ring_gather_rotated(): f = lax.ppermute(f, axis, fwd)  17.9 us
    ppermute x8, waiting for transfers between devices, ring_gather_rotated(): f = lax.ppermute(f, axis, fwd)  17 us
    all_to_all x1, starting transfers between devices, per_device(): lax.all_to_all(dy_slots, 'expert', split_axis=0, concat_axis=0, tiled=True)  10.6 us
    all_to_all x1, starting transfers between devices, per_device(): lax.all_to_all(prob_sum.astype(jnp.bfloat16).reshape(n_expert, capacity),...  9.96 us
  transfers between devices with their start and end apart: 22, of which 9 were waited for; matrix products, arithmetic and copies ran while one was open for 30% of the time, Pallas kernels for 0%

profile of v2, /device:TPU:1, one launch (start us, length us, event | category | flops | bytes accessed | tf_op | source)
XLA Modules:
  0.0 277.5 jit_solution(16109185971472932869)
XLA Ops:
  10.6 4.4 %collective-permute-start.7 = (bf16[2,128,768]{2,1,0:T(8,128)(2,1)}, bf16[2,128,768]{2,1,0:T(8,128)(2,1)S(1)}, u32[]{:S(2)}, u32[]{:S(2)}) collective-permute-start(bf16[2,128,768]{2,1,0:T(8,128)(2,1)} %get-tuple-element.9), channel_id=1, source_target_pairs={{0,32},{32,64},{64,96},{96,128},{128,160},{160,192},{192,224},{224... | collective-permute-start | bytes 1179656 | tf_op jit(solution)/shard_map/ppermute | solution.py:18
  20.4 2.5 gather_fusion
  23.6 8.0 %all-to-all-start = ((bf16[32,1,10]{2,1,0:T(2,128)(2,1)}), bf16[32,1,10]{2,1,0:T(2,128)(2,1)S(1)}, u32[]{:S(2)}, u32[]{:S(2)}) async-start(bf16[32,1,10]{2,1,0:T(2,128)(2,1)} %all_to_all.25), calls=%async_computation | async-start | bytes 32768 | tf_op jit(solution)/shard_map/all_to_all | solution.py:60
  31.7 2.4 gather_fusion.2
  35.8 2.7 all-to-all-done
  38.6 4.7 %all-to-all-start.2 = ((bf16[32,10,2048]{2,1,0:T(8,128)(2,1)}), bf16[32,10,2048]{2,1,0:T(8,128)(2,1)S(1)}, u32[]{:S(2)}, u32[]{:S(2)}) async-start(bf16[32,10,2048]{2,1,0:T(8,128)(2,1)} %reshape.123), calls=%async_computation.2 | async-start | bytes 4194304 | tf_op jit(solution)/shard_map/all_to_all | solution.py:58
  43.2 9.2 %collective-permute-start = (bf16[2,128,768]{2,1,0:T(8,128)(2,1)}, bf16[2,128,768]{2,1,0:T(8,128)(2,1)S(1)}, u32[]{:S(2)}, u32[]{:S(2)}) collective-permute-start(bf16[2,128,768]{2,1,0:T(8,128)(2,1)} %get-tuple-element.9), channel_id=1, source_target_pairs={{0,480},{32,0},{64,32},{96,64},{128,96},{160,128},{192,160},{224,1... | collective-permute-start | bytes 1179656 | tf_op jit(solution)/shard_map/ppermute | solution.py:21
  52.5 1.9 collective-permute-start.8
  54.4 14.4 %collective-permute-done = bf16[2,128,768]{2,1,0:T(8,128)(2,1)S(1)} collective-permute-done((bf16[2,128,768]{2,1,0:T(8,128)(2,1)}, bf16[2,128,768]{2,1,0:T(8,128)(2,1)S(1)}, u32[]{:S(2)}, u32[]{:S(2)}) %collective-permute-start) | collective-permute-done | bytes 393248 | tf_op jit(solution)/shard_map/ppermute | solution.py:21
  68.8 5.3 %collective-permute-start.1 = (bf16[2,128,768]{2,1,0:T(8,128)(2,1)S(1)}, bf16[2,128,768]{2,1,0:T(8,128)(2,1)S(1)}, u32[]{:S(2)}, u32[]{:S(2)}) collective-permute-start(bf16[2,128,768]{2,1,0:T(8,128)(2,1)S(1)} %collective-permute-done), channel_id=1, source_target_pairs={{0,480},{32,0},{64,32},{96,64},{128,96},{160,128},{192,160},{224,1... | collective-permute-start | bytes 1179656 | tf_op jit(solution)/shard_map/ppermute | solution.py:21
  74.1 1.9 collective-permute-start.9
  76.1 13.0 %collective-permute-done.1 = bf16[2,128,768]{2,1,0:T(8,128)(2,1)S(1)} collective-permute-done((bf16[2,128,768]{2,1,0:T(8,128)(2,1)S(1)}, bf16[2,128,768]{2,1,0:T(8,128)(2,1)S(1)}, u32[]{:S(2)}, u32[]{:S(2)}) %collective-permute-start.1) | collective-permute-done | bytes 393248 | tf_op jit(solution)/shard_map/ppermute | solution.py:21
  89.0 5.4 %collective-permute-start.2 = (bf16[2,128,768]{2,1,0:T(8,128)(2,1)S(1)}, bf16[2,128,768]{2,1,0:T(8,128)(2,1)}, u32[]{:S(2)}, u32[]{:S(2)}) collective-permute-start(bf16[2,128,768]{2,1,0:T(8,128)(2,1)S(1)} %collective-permute-done.1), channel_id=1, source_target_pairs={{0,480},{32,0},{64,32},{96,64},{128,96},{160,128},{192,160},{224,1... | collective-permute-start | bytes 1179656 | tf_op jit(solution)/shard_map/ppermute | solution.py:21
  94.8 1.9 collective-permute-start.10
  96.7 5.8 %collective-permute-done.2 = bf16[2,128,768]{2,1,0:T(8,128)(2,1)} collective-permute-done((bf16[2,128,768]{2,1,0:T(8,128)(2,1)S(1)}, bf16[2,128,768]{2,1,0:T(8,128)(2,1)}, u32[]{:S(2)}, u32[]{:S(2)}) %collective-permute-start.2) | collective-permute-done | bytes 393248 | tf_op jit(solution)/shard_map/ppermute | solution.py:21
  102.5 5.4 %collective-permute-start.3 = (bf16[2,128,768]{2,1,0:T(8,128)(2,1)}, bf16[2,128,768]{2,1,0:T(8,128)(2,1)}, u32[]{:S(2)}, u32[]{:S(2)}) collective-permute-start(bf16[2,128,768]{2,1,0:T(8,128)(2,1)} %collective-permute-done.2), channel_id=1, source_target_pairs={{0,480},{32,0},{64,32},{96,64},{128,96},{160,128},{192,160},{224,1... | collective-permute-start | bytes 1179656 | tf_op jit(solution)/shard_map/ppermute | solution.py:21
  108.0 3.0 %gather_fusion.1 = bf16[320,2048]{1,0:T(8,128)(2,1)} fusion(bf16[129,2048]{1,0:T(8,128)(2,1)S(1)} %concatenate.20, s32[1024]{0:T(1024)S(1)} %get-tuple-element.17), kind=kCustom, calls=%fused_computation.1 | custom fusion | bytes 2622720 | tf_op jit(solution)/shard_map/gather | solution.py:55
  111.0 3.4 %reshape.122 = bf16[32,10,2048]{2,1,0:T(8,128)(2,1)} reshape(bf16[320,2048]{1,0:T(8,128)(2,1)} %gather_fusion.1) | data formatting | bytes 2621440 | tf_op jit(solution)/shard_map/reshape | solution.py:55
  114.4 10.6 %all-to-all-start.1 = ((bf16[32,10,2048]{2,1,0:T(8,128)(2,1)}), bf16[32,10,2048]{2,1,0:T(8,128)(2,1)}, u32[]{:S(2)}, u32[]{:S(2)}) async-start(bf16[32,10,2048]{2,1,0:T(8,128)(2,1)} %reshape.122), calls=%async_computation.1 | async-start | bytes 4194304 | tf_op jit(solution)/shard_map/all_to_all | solution.py:59
  125.1 1.9 collective-permute-start.11
  127.0 4.6 %collective-permute-start.4 = (bf16[2,128,768]{2,1,0:T(8,128)(2,1)}, bf16[2,128,768]{2,1,0:T(8,128)(2,1)}, u32[]{:S(2)}, u32[]{:S(2)}) collective-permute-start(bf16[2,128,768]{2,1,0:T(8,128)(2,1)} %collective-permute-done.3), channel_id=1, source_target_pairs={{0,480},{32,0},{64,32},{96,64},{128,96},{160,128},{192,160},{224,1... | collective-permute-start | bytes 1179656 | tf_op jit(solution)/shard_map/ppermute | solution.py:21
  131.6 7.3 %collective-permute-done.11 = bf16[2,128,768]{2,1,0:T(8,128)(2,1)S(1)} collective-permute-done((bf16[2,128,768]{2,1,0:T(8,128)(2,1)}, bf16[2,128,768]{2,1,0:T(8,128)(2,1)S(1)}, u32[]{:S(2)}, u32[]{:S(2)}) %collective-permute-start.11) | collective-permute-done | bytes 393248 | tf_op jit(solution)/shard_map/ppermute | solution.py:18
  138.8 1.9 collective-permute-start.12
  140.8 4.6 %collective-permute-start.5 = (bf16[2,128,768]{2,1,0:T(8,128)(2,1)}, bf16[2,128,768]{2,1,0:T(8,128)(2,1)}, u32[]{:S(2)}, u32[]{:S(2)}) collective-permute-start(bf16[2,128,768]{2,1,0:T(8,128)(2,1)} %collective-permute-done.4), channel_id=1, source_target_pairs={{0,480},{32,0},{64,32},{96,64},{128,96},{160,128},{192,160},{224,1... | collective-permute-start | bytes 1179656 | tf_op jit(solution)/shard_map/ppermute | solution.py:21
  145.4 6.3 %collective-permute-done.12 = bf16[2,128,768]{2,1,0:T(8,128)(2,1)} collective-permute-done((bf16[2,128,768]{2,1,0:T(8,128)(2,1)S(1)}, bf16[2,128,768]{2,1,0:T(8,128)(2,1)}, u32[]{:S(2)}, u32[]{:S(2)}) %collective-permute-start.12) | collective-permute-done | bytes 393248 | tf_op jit(solution)/shard_map/ppermute | solution.py:18
  151.6 1.9 collective-permute-start.13
  155.3 4.6 %collective-permute-start.6 = (bf16[2,128,768]{2,1,0:T(8,128)(2,1)}, bf16[2,128,768]{2,1,0:T(8,128)(2,1)S(1)}, u32[]{:S(2)}, u32[]{:S(2)}) collective-permute-start(bf16[2,128,768]{2,1,0:T(8,128)(2,1)} %collective-permute-done.5), channel_id=1, source_target_pairs={{0,480},{32,0},{64,32},{96,64},{128,96},{160,128},{192,160},{224,1... | collective-permute-start | bytes 1179656 | tf_op jit(solution)/shard_map/ppermute | solution.py:21
  163.0 2.5 reshape.130
  165.5 2.1 collective-permute-start.14
  167.6 1.8 constant_dynamic-update-slice_fusion.13
  171.2 1.9 constant_dynamic-update-slice_fusion.11
  173.8 3.2 %collective-permute-done.14 = bf16[2,128,768]{2,1,0:T(8,128)(2,1)S(1)} collective-permute-done((bf16[2,128,768]{2,1,0:T(8,128)(2,1)}, bf16[2,128,768]{2,1,0:T(8,128)(2,1)S(1)}, u32[]{:S(2)}, u32[]{:S(2)}) %collective-permute-start.14) | collective-permute-done | bytes 393248 | tf_op jit(solution)/shard_map/ppermute | solution.py:18
  177.8 1.8 constant_dynamic-update-slice_fusion.8
  179.6 1.8 constant_dynamic-update-slice_fusion.7
  183.9 1.8 constant_dynamic-update-slice_fusion.4
  187.3 3.6 %fusion.9 = f32[320,768]{1,0:T(8,128)S(1)} fusion(bf16[2,2048,768]{2,1,0:T(8,128)(2,1)} %constant_dynamic-update-slice_fusion.2, s32[]{:T(128)S(6)} %select_n.51, bf16[320,2048]{1,0:T(8,128)(2,1)S(1)} %copy-done), kind=kOutput, calls=%fused_computation.18 | convolution fusion | flops 1009254400 | bytes 5439492 | tf_op jit(solution)/shard_map/dot_general | solution.py:72
  191.0 2.5 multiply_convert_fusion.3
  193.6 3.6 %convolution_convert_fusion = bf16[2048,768]{1,0:T(8,128)(2,1)} fusion(bf16[320,768]{1,0:T(8,128)(2,1)S(1)} %get-tuple-element.15, f32[320,2048]{1,0:T(8,128)S(1)} %reshape.130, f32[320]{0:T(512)S(1)} %reshape.131), kind=kOutput, calls=%fused_computation.7 | convolution fusion | flops 1009516544 | bytes 6259968 | tf_op jit(solution)/shard_map/dot_general | solution.py:92
  197.2 3.3 %multiply_convert_fusion = bf16[32,10,2048]{2,1,0:T(8,128)(2,1)} fusion(f32[32,10]{1,0:T(8,128)S(1)} %bitcast.47, bf16[32,10,2048]{2,1,0:T(8,128)(2,1)} %all-to-all-done.1), kind=kLoop, calls=%fused_computation.6 | loop fusion | flops 1966080 | bytes 2622720 | tf_op jit(solution)/shard_map/convert_element_type | solution.py:65
  200.5 3.6 %convert_element_type.80 = bf16[320,2048]{1,0:T(8,128)(2,1)} reshape(bf16[32,10,2048]{2,1,0:T(8,128)(2,1)} %multiply_convert_fusion) | data formatting | bytes 2621440 | tf_op jit(solution)/shard_map/convert_element_type | solution.py:65
  204.1 3.2 %fusion.11 = bf16[320]{0:T(512)(128)(2,1)S(1)} fusion(f32[320,2048]{1,0:T(8,128)S(1)} %reshape.130, bf16[320,768]{1,0:T(8,128)(2,1)S(1)} %get-tuple-element.15, bf16[1,2048,768]{2,1,0:T(8,128)(2,1)} %all-gather.2.cloned.1.call-done), kind=kOutput, calls=%fused_computation.25 | convolution fusion | flops 1007943360 | bytes 6259328 | tf_op jit(solution)/shard_map/dot_general | solution.py:78
  208.1 10.0 %all-to-all-start.4 = ((bf16[32,1,10]{2,1,0:T(2,128)(2,1)}), bf16[32,1,10]{2,1,0:T(2,128)(2,1)S(1)}, u32[]{:S(2)}, u32[]{:S(2)}) async-start(bf16[32,1,10]{2,1,0:T(2,128)(2,1)} %convert_element_type.96), calls=%async_computation.4 | async-start | bytes 32768 | tf_op jit(solution)/shard_map/all_to_all | solution.py:108
  218.1 3.6 %fusion.2 = f32[320,768]{1,0:T(8,128)S(1)} fusion(bf16[320,2048]{1,0:T(8,128)(2,1)} %convert_element_type.80, bf16[1,2048,768]{2,1,0:T(8,128)(2,1)} %all-gather.2.cloned.1.call-done), kind=kOutput, calls=%fused_computation.12 | convolution fusion | flops 1006632960 | bytes 5439488 | tf_op jit(solution)/shard_map/dot_general | solution.py:79
  221.7 3.3 %fusion.7 = f32[320,2048]{1,0:T(8,128)S(1)} fusion(bf16[2,2048,768]{2,1,0:T(8,128)(2,1)} %constant_dynamic-update-slice_fusion.2, f32[320,768]{1,0:T(8,128)S(1)} %fusion.2, f32[320,768]{1,0:T(8,128)S(1)} %copy-done.13), kind=kOutput, calls=%fused_computation.16 | convolution fusion | flops 1008107520 | bytes 7733248 | tf_op jit(solution)/shard_map/dot_general | solution.py:88
  228.8 7.4 %all-to-all-start.3 = ((bf16[32,10,2048]{2,1,0:T(8,128)(2,1)}), bf16[32,10,2048]{2,1,0:T(8,128)(2,1)S(1)}, u32[]{:S(2)}, u32[]{:S(2)}) async-start(bf16[32,10,2048]{2,1,0:T(8,128)(2,1)} %reshape.125), calls=%async_computation.3 | async-start | bytes 4194304 | tf_op jit(solution)/shard_map/all_to_all | solution.py:101
  236.3 1.9 gather_fusion.4
  239.0 25.4 %all-to-all-done.3 = bf16[32,10,2048]{2,1,0:T(8,128)(2,1)S(1)} async-done(((bf16[32,10,2048]{2,1,0:T(8,128)(2,1)}), bf16[32,10,2048]{2,1,0:T(8,128)(2,1)S(1)}, u32[]{:S(2)}, u32[]{:S(2)}) %all-to-all-start.3) | async-done | bytes 1310752 | tf_op jit(solution)/shard_map/all_to_all | solution.py:101
  267.1 3.6 %reduce_sum.34 = bf16[128,2048]{1,0:T(8,128)(2,1)} reduce(bf16[128,2,2048]{2,1,0:T(2,128)(2,1)S(1)} %gather.21, bf16[]{:T(256)} %constant.55.clone.1), dimensions={1}, to_apply=%region_4.5 | reduce | flops 262144 | bytes 1572866 | tf_op jit(solution)/shard_map/reduce_sum | solution.py:119
  (106 shorter events, 32.1 us)
Async XLA Ops:
  7.2 24.5 %copy-start.1 = (bf16[128,2048]{1,0:T(8,128)(2,1)S(1)}, bf16[128,2048]{1,0:T(8,128)(2,1)}, u32[]{:S(2)}) copy-start(bf16[128,2048]{1,0:T(8,128)(2,1)} %param.7) | copy-start | bytes 1572868
  7.2 197.0 %all-gather.2.cloned.1.call-start = ((), (), s32[]{:S(2)}) async-start(), calls=%async_computation.6 | async-start | bytes 3342336 | tf_op jit(solution)/shard_map/all_gather | solution.py:77
  10.6 41.8 %collective-permute-start.7 = (bf16[2,128,768]{2,1,0:T(8,128)(2,1)}, bf16[2,128,768]{2,1,0:T(8,128)(2,1)S(1)}, u32[]{:S(2)}, u32[]{:S(2)}) collective-permute-start(bf16[2,128,768]{2,1,0:T(8,128)(2,1)} %get-tuple-element.9), channel_id=1, source_target_pairs={{0,32},{32,64},{64,96},{96,128},{128,160},{160,192},{192,224},{224... | collective-permute-start | bytes 1179656 | tf_op jit(solution)/shard_map/ppermute | solution.py:18
  23.6 14.9 %all-to-all-start = ((bf16[32,1,10]{2,1,0:T(2,128)(2,1)}), bf16[32,1,10]{2,1,0:T(2,128)(2,1)S(1)}, u32[]{:S(2)}, u32[]{:S(2)}) async-start(bf16[32,1,10]{2,1,0:T(2,128)(2,1)} %all_to_all.25), calls=%async_computation | async-start | bytes 32768 | tf_op jit(solution)/shard_map/all_to_all | solution.py:60
  34.2 73.7 %copy-start.2 = (bf16[128,2048]{1,0:T(8,128)(2,1)S(1)}, bf16[128,2048]{1,0:T(8,128)(2,1)}, u32[]{:S(2)}) copy-start(bf16[128,2048]{1,0:T(8,128)(2,1)} %param.8) | copy-start | bytes 1572868
  38.6 75.8 %all-to-all-start.2 = ((bf16[32,10,2048]{2,1,0:T(8,128)(2,1)}), bf16[32,10,2048]{2,1,0:T(8,128)(2,1)S(1)}, u32[]{:S(2)}, u32[]{:S(2)}) async-start(bf16[32,10,2048]{2,1,0:T(8,128)(2,1)} %reshape.123), calls=%async_computation.2 | async-start | bytes 4194304 | tf_op jit(solution)/shard_map/all_to_all | solution.py:58
  43.2 25.5 %collective-permute-start = (bf16[2,128,768]{2,1,0:T(8,128)(2,1)}, bf16[2,128,768]{2,1,0:T(8,128)(2,1)S(1)}, u32[]{:S(2)}, u32[]{:S(2)}) collective-permute-start(bf16[2,128,768]{2,1,0:T(8,128)(2,1)} %get-tuple-element.9), channel_id=1, source_target_pairs={{0,480},{32,0},{64,32},{96,64},{128,96},{160,128},{192,160},{224,1... | collective-permute-start | bytes 1179656 | tf_op jit(solution)/shard_map/ppermute | solution.py:21
  52.5 50.0 %copy-start.3 = (bf16[2,128,768]{2,1,0:T(8,128)(2,1)}, bf16[2,128,768]{2,1,0:T(8,128)(2,1)S(1)}, u32[]{:S(2)}) copy-start(bf16[2,128,768]{2,1,0:T(8,128)(2,1)S(1)} %collective-permute-done.7) | copy-start | bytes 1179652
  52.5 21.6 %collective-permute-start.8 = (bf16[2,128,768]{2,1,0:T(8,128)(2,1)S(1)}, bf16[2,128,768]{2,1,0:T(8,128)(2,1)S(1)}, u32[]{:S(2)}, u32[]{:S(2)}) collective-permute-start(bf16[2,128,768]{2,1,0:T(8,128)(2,1)S(1)} %collective-permute-done.7), channel_id=1, source_target_pairs={{0,32},{32,64},{64,96},{96,128},{128,160},{160,192},{192,224},{224... | collective-permute-start | bytes 1179656 | tf_op jit(solution)/shard_map/ppermute | solution.py:18
  68.8 33.7 %copy-start.7 = (bf16[2,128,768]{2,1,0:T(8,128)(2,1)}, bf16[2,128,768]{2,1,0:T(8,128)(2,1)S(1)}, u32[]{:S(2)}) copy-start(bf16[2,128,768]{2,1,0:T(8,128)(2,1)S(1)} %collective-permute-done) | copy-start | bytes 1179652
  68.8 20.2 %collective-permute-start.1 = (bf16[2,128,768]{2,1,0:T(8,128)(2,1)S(1)}, bf16[2,128,768]{2,1,0:T(8,128)(2,1)S(1)}, u32[]{:S(2)}, u32[]{:S(2)}) collective-permute-start(bf16[2,128,768]{2,1,0:T(8,128)(2,1)S(1)} %collective-permute-done), channel_id=1, source_target_pairs={{0,480},{32,0},{64,32},{96,64},{128,96},{160,128},{192,160},{224,1... | collective-permute-start | bytes 1179656 | tf_op jit(solution)/shard_map/ppermute | solution.py:21
  74.1 28.3 %copy-start.5 = (bf16[2,128,768]{2,1,0:T(8,128)(2,1)}, bf16[2,128,768]{2,1,0:T(8,128)(2,1)S(1)}, u32[]{:S(2)}) copy-start(bf16[2,128,768]{2,1,0:T(8,128)(2,1)S(1)} %collective-permute-done.8) | copy-start | bytes 1179652
  74.1 20.6 %collective-permute-start.9 = (bf16[2,128,768]{2,1,0:T(8,128)(2,1)S(1)}, bf16[2,128,768]{2,1,0:T(8,128)(2,1)}, u32[]{:S(2)}, u32[]{:S(2)}) collective-permute-start(bf16[2,128,768]{2,1,0:T(8,128)(2,1)S(1)} %collective-permute-done.8), channel_id=1, source_target_pairs={{0,32},{32,64},{64,96},{96,128},{128,160},{160,192},{192,224},{224... | collective-permute-start | bytes 1179656 | tf_op jit(solution)/shard_map/ppermute | solution.py:18
  89.0 13.5 %copy-start.9 = (bf16[2,128,768]{2,1,0:T(8,128)(2,1)}, bf16[2,128,768]{2,1,0:T(8,128)(2,1)S(1)}, u32[]{:S(2)}) copy-start(bf16[2,128,768]{2,1,0:T(8,128)(2,1)S(1)} %collective-permute-done.1) | copy-start | bytes 1179652
  89.0 13.4 %collective-permute-start.2 = (bf16[2,128,768]{2,1,0:T(8,128)(2,1)S(1)}, bf16[2,128,768]{2,1,0:T(8,128)(2,1)}, u32[]{:S(2)}, u32[]{:S(2)}) collective-permute-start(bf16[2,128,768]{2,1,0:T(8,128)(2,1)S(1)} %collective-permute-done.1), channel_id=1, source_target_pairs={{0,480},{32,0},{64,32},{96,64},{128,96},{160,128},{192,160},{224,1... | collective-permute-start | bytes 1179656 | tf_op jit(solution)/shard_map/ppermute | solution.py:21
  94.8 30.3 %collective-permute-start.10 = (bf16[2,128,768]{2,1,0:T(8,128)(2,1)}, bf16[2,128,768]{2,1,0:T(8,128)(2,1)}, u32[]{:S(2)}, u32[]{:S(2)}) collective-permute-start(bf16[2,128,768]{2,1,0:T(8,128)(2,1)} %collective-permute-done.9), channel_id=1, source_target_pairs={{0,32},{32,64},{64,96},{96,128},{128,160},{160,192},{192,224},{224... | collective-permute-start | bytes 1179656 | tf_op jit(solution)/shard_map/ppermute | solution.py:18
  102.5 24.5 %collective-permute-start.3 = (bf16[2,128,768]{2,1,0:T(8,128)(2,1)}, bf16[2,128,768]{2,1,0:T(8,128)(2,1)}, u32[]{:S(2)}, u32[]{:S(2)}) collective-permute-start(bf16[2,128,768]{2,1,0:T(8,128)(2,1)} %collective-permute-done.2), channel_id=1, source_target_pairs={{0,480},{32,0},{64,32},{96,64},{128,96},{160,128},{192,160},{224,1... | collective-permute-start | bytes 1179656 | tf_op jit(solution)/shard_map/ppermute | solution.py:21
  111.0 42.7 %copy-start.8 = (bf16[2,128,768]{2,1,0:T(8,128)(2,1)S(1)}, bf16[2,128,768]{2,1,0:T(8,128)(2,1)}, u32[]{:S(2)}) copy-start(bf16[2,128,768]{2,1,0:T(8,128)(2,1)} %copy-done.7) | copy-start | bytes 1179652
  114.4 40.1 %copy-start.10 = (bf16[2,128,768]{2,1,0:T(8,128)(2,1)S(1)}, bf16[2,128,768]{2,1,0:T(8,128)(2,1)}, u32[]{:S(2)}) copy-start(bf16[2,128,768]{2,1,0:T(8,128)(2,1)} %copy-done.9) | copy-start | bytes 1179652
  114.4 48.6 %all-to-all-start.1 = ((bf16[32,10,2048]{2,1,0:T(8,128)(2,1)}), bf16[32,10,2048]{2,1,0:T(8,128)(2,1)}, u32[]{:S(2)}, u32[]{:S(2)}) async-start(bf16[32,10,2048]{2,1,0:T(8,128)(2,1)} %reshape.122), calls=%async_computation.1 | async-start | bytes 4194304 | tf_op jit(solution)/shard_map/all_to_all | solution.py:59
  125.0 145.7 %reduce-scatter.2.cloned.1.call-start = ((), (), s32[]{:S(2)}) async-start(), calls=%async_computation.7 | async-start | bytes 3342336 | tf_op jit(solution)/shard_map/reduce_scatter | solution.py:91
  125.1 13.8 %collective-permute-start.11 = (bf16[2,128,768]{2,1,0:T(8,128)(2,1)}, bf16[2,128,768]{2,1,0:T(8,128)(2,1)S(1)}, u32[]{:S(2)}, u32[]{:S(2)}) collective-permute-start(bf16[2,128,768]{2,1,0:T(8,128)(2,1)} %collective-permute-done.10), channel_id=1, source_target_pairs={{0,32},{32,64},{64,96},{96,128},{128,160},{160,192},{192,224},{224... | collective-permute-start | bytes 1179656 | tf_op jit(solution)/shard_map/ppermute | solution.py:18
  127.0 13.8 %collective-permute-start.4 = (bf16[2,128,768]{2,1,0:T(8,128)(2,1)}, bf16[2,128,768]{2,1,0:T(8,128)(2,1)}, u32[]{:S(2)}, u32[]{:S(2)}) collective-permute-start(bf16[2,128,768]{2,1,0:T(8,128)(2,1)} %collective-permute-done.3), channel_id=1, source_target_pairs={{0,480},{32,0},{64,32},{96,64},{128,96},{160,128},{192,160},{224,1... | collective-permute-start | bytes 1179656 | tf_op jit(solution)/shard_map/ppermute | solution.py:21
  138.8 12.8 %collective-permute-start.12 = (bf16[2,128,768]{2,1,0:T(8,128)(2,1)S(1)}, bf16[2,128,768]{2,1,0:T(8,128)(2,1)}, u32[]{:S(2)}, u32[]{:S(2)}) collective-permute-start(bf16[2,128,768]{2,1,0:T(8,128)(2,1)S(1)} %collective-permute-done.11), channel_id=1, source_target_pairs={{0,32},{32,64},{64,96},{96,128},{128,160},{160,192},{192,224},{224... | collective-permute-start | bytes 1179656 | tf_op jit(solution)/shard_map/ppermute | solution.py:18
  140.8 14.6 %collective-permute-start.5 = (bf16[2,128,768]{2,1,0:T(8,128)(2,1)}, bf16[2,128,768]{2,1,0:T(8,128)(2,1)}, u32[]{:S(2)}, u32[]{:S(2)}) collective-permute-start(bf16[2,128,768]{2,1,0:T(8,128)(2,1)} %collective-permute-done.4), channel_id=1, source_target_pairs={{0,480},{32,0},{64,32},{96,64},{128,96},{160,128},{192,160},{224,1... | collective-permute-start | bytes 1179656 | tf_op jit(solution)/shard_map/ppermute | solution.py:21
  151.6 13.8 %collective-permute-start.13 = (bf16[2,128,768]{2,1,0:T(8,128)(2,1)}, bf16[2,128,768]{2,1,0:T(8,128)(2,1)}, u32[]{:S(2)}, u32[]{:S(2)}) collective-permute-start(bf16[2,128,768]{2,1,0:T(8,128)(2,1)} %collective-permute-done.12), channel_id=1, source_target_pairs={{0,32},{32,64},{64,96},{96,128},{128,160},{160,192},{192,224},{224... | collective-permute-start | bytes 1179656 | tf_op jit(solution)/shard_map/ppermute | solution.py:18
  155.3 17.7 %collective-permute-start.6 = (bf16[2,128,768]{2,1,0:T(8,128)(2,1)}, bf16[2,128,768]{2,1,0:T(8,128)(2,1)S(1)}, u32[]{:S(2)}, u32[]{:S(2)}) collective-permute-start(bf16[2,128,768]{2,1,0:T(8,128)(2,1)} %collective-permute-done.5), channel_id=1, source_target_pairs={{0,480},{32,0},{64,32},{96,64},{128,96},{160,128},{192,160},{224,1... | collective-permute-start | bytes 1179656 | tf_op jit(solution)/shard_map/ppermute | solution.py:21
  165.5 11.5 %collective-permute-start.14 = (bf16[2,128,768]{2,1,0:T(8,128)(2,1)}, bf16[2,128,768]{2,1,0:T(8,128)(2,1)S(1)}, u32[]{:S(2)}, u32[]{:S(2)}) collective-permute-start(bf16[2,128,768]{2,1,0:T(8,128)(2,1)} %collective-permute-done.13), channel_id=1, source_target_pairs={{0,32},{32,64},{64,96},{96,128},{128,160},{160,192},{192,224},{224... | collective-permute-start | bytes 1179656 | tf_op jit(solution)/shard_map/ppermute | solution.py:18
  171.2 14.5 %copy-start.6 = (bf16[2,128,768]{2,1,0:T(8,128)(2,1)S(1)}, bf16[2,128,768]{2,1,0:T(8,128)(2,1)}, u32[]{:S(2)}) copy-start(bf16[2,128,768]{2,1,0:T(8,128)(2,1)} %copy-done.5) | copy-start | bytes 1179652
  173.0 13.5 %copy-start.4 = (bf16[2,128,768]{2,1,0:T(8,128)(2,1)S(1)}, bf16[2,128,768]{2,1,0:T(8,128)(2,1)}, u32[]{:S(2)}) copy-start(bf16[2,128,768]{2,1,0:T(8,128)(2,1)} %copy-done.3) | copy-start | bytes 1179652
  173.8 13.5 %copy-start = (bf16[320,2048]{1,0:T(8,128)(2,1)S(1)}, bf16[320,2048]{1,0:T(8,128)(2,1)}, u32[]{:S(2)}) copy-start(bf16[320,2048]{1,0:T(8,128)(2,1)} %reshape.124) | copy-start | bytes 3932164
  187.3 3.7 %copy-start.11 = (bf16[2,2048,768]{2,1,0:T(8,128)(2,1)S(1)}, bf16[2,2048,768]{2,1,0:T(8,128)(2,1)}, u32[]{:S(2)}) copy-start(bf16[2,2048,768]{2,1,0:T(8,128)(2,1)} %constant_dynamic-update-slice_fusion.2) | copy-start | bytes 18874372
  191.0 2.5 copy-start.12
  208.1 20.7 %all-to-all-start.4 = ((bf16[32,1,10]{2,1,0:T(2,128)(2,1)}), bf16[32,1,10]{2,1,0:T(2,128)(2,1)S(1)}, u32[]{:S(2)}, u32[]{:S(2)}) async-start(bf16[32,1,10]{2,1,0:T(2,128)(2,1)} %convert_element_type.96), calls=%async_computation.4 | async-start | bytes 32768 | tf_op jit(solution)/shard_map/all_to_all | solution.py:108
  218.0 3.7 %copy-start.13 = (f32[320,768]{1,0:T(8,128)S(1)}, f32[320,768]{1,0:T(8,128)}, u32[]{:S(2)}) copy-start(f32[320,768]{1,0:T(8,128)} %copy-done.12) | copy-start | bytes 2949124
  218.1 7.0 %slice-start = ((s8[6291456]{0:T(1024)(128)(4,1)}), s8[4194304]{0:T(1024)(128)(4,1)S(1)}, s32[]{:S(2)}) async-start(s8[6291456]{0:T(1024)(128)(4,1)} %bitcast.48), calls=%async_computation.8 | async-start | bytes 8388608
  221.7 3.4 %slice-start.1 = ((s8[6291456]{0:T(1024)(128)(4,1)}), s8[2097152]{0:T(1024)(128)(4,1)S(1)}, s32[]{:S(2)}) async-start(s8[6291456]{0:T(1024)(128)(4,1)} %bitcast.48), calls=%async_computation.9 | async-start | bytes 4194304
  221.7 3.4 %copy-start.14 = (f32[320,768]{1,0:T(8,128)S(1)}, f32[320,768]{1,0:T(8,128)}, u32[]{:S(2)}) copy-start(f32[320,768]{1,0:T(8,128)} %get-tuple-element.16) | copy-start | bytes 2949124
  228.8 35.7 %all-to-all-start.3 = ((bf16[32,10,2048]{2,1,0:T(8,128)(2,1)}), bf16[32,10,2048]{2,1,0:T(8,128)(2,1)S(1)}, u32[]{:S(2)}, u32[]{:S(2)}) async-start(bf16[32,10,2048]{2,1,0:T(8,128)(2,1)} %reshape.125), calls=%async_computation.3 | async-start | bytes 4194304 | tf_op jit(solution)/shard_map/all_to_all | solution.py:101
Sparse Core Ops, SparseCore 0:
  15.1 80.2 all-gather.1
  197.3 68.4 reduce-scatter.1

commit v3 on v2

v3 whole, which is shorter than its diff:
```python
import jax
import jax.numpy as jnp
from jax import lax
from jax.sharding import PartitionSpec as P


def ring_gather_pieces(shard, axis):
    n = lax.axis_size(axis)
    fwd = [(m, (m + 1) % n) for m in range(n)]
    bwd = [(m, (m - 1) % n) for m in range(n)]
    nf = n // 2
    nb = (n - 1) // 2
    f = shard
    b = shard
    got_f = {}
    got_b = {}
    for s in range(1, nf + 1):
        f = lax.ppermute(f, axis, fwd)
        got_f[s] = f
        if s <= nb:
            b = lax.ppermute(b, axis, bwd)
            got_b[s] = b
    return [shard] + [got_b[k] for k in range(1, nb + 1)] + [got_f[n - k] for k in range(nb + 1, n)]


def roll_cols(a, shift, width):
    doubled = jnp.concatenate([a, a], axis=1)
    return lax.dynamic_slice_in_dim(doubled, shift % width, width, axis=1)


def per_device(x_tokens, grad_out, expert_ids, route_probs, w_gate, w_up, w_down):
    tok_count, model_width = x_tokens.shape
    top_count = expert_ids.shape[1]
    n_expert = lax.axis_size("expert")
    n_dp = lax.axis_size("dp")
    capacity = tok_count * top_count * 5 // (4 * n_expert)
    slot_count = n_expert * capacity
    routes = tok_count * top_count
    flat_ids = expert_ids.reshape(routes)
    onehot = (flat_ids[:, None] == jnp.arange(n_expert, dtype=jnp.int32)).astype(jnp.int32)
    route_rank = jnp.sum((jnp.cumsum(onehot, axis=0) - onehot) * onehot, axis=1)
    target = flat_ids * capacity + route_rank
    source = (
        jnp.full((slot_count,), routes, jnp.int32)
        .at[target]
        .set(jnp.arange(routes, dtype=jnp.int32))
    )
    token_of = jnp.where(source < routes, source // top_count, tok_count)
    lane = 128
    p_col = jnp.concatenate([route_probs.reshape(routes), jnp.zeros((1,), jnp.float32)]).astype(
        jnp.bfloat16
    )[source]
    p_block = jnp.zeros((slot_count, lane), jnp.bfloat16).at[:, 0].set(p_col)
    x_padded = jnp.concatenate([x_tokens, jnp.zeros((1, model_width), jnp.bfloat16)], axis=0)
    dy_padded = jnp.concatenate([grad_out, jnp.zeros((1, model_width), jnp.bfloat16)], axis=0)
    packed = jnp.concatenate([x_padded[token_of], dy_padded[token_of], p_block], axis=1)
    arrived = lax.all_to_all(
        packed.reshape(n_expert, capacity, 2 * model_width + lane),
        "expert",
        split_axis=0,
        concat_axis=0,
        tiled=True,
    ).reshape(slot_count, 2 * model_width + lane)
    in_rows = arrived[:, :model_width]
    dy_rows = arrived[:, model_width : 2 * model_width]
    p_rows = arrived[:, 2 * model_width].astype(jnp.float32)
    scaled = (p_rows[:, None] * dy_rows.astype(jnp.float32)).astype(jnp.bfloat16)

    dp_index = lax.axis_index("dp")
    shard_rows = w_gate.shape[1]
    pieces = ring_gather_pieces(jnp.stack([w_gate[0], w_up[0]]), "dp")
    in_rot = roll_cols(in_rows, dp_index * shard_rows, model_width)
    gate_pre = None
    up_pre = None
    for k, piece in enumerate(pieces):
        cols = in_rot[:, k * shard_rows : (k + 1) * shard_rows]
        g = jnp.dot(cols, piece[0], preferred_element_type=jnp.float32)
        u = jnp.dot(cols, piece[1], preferred_element_type=jnp.float32)
        gate_pre = g if gate_pre is None else gate_pre + g
        up_pre = u if up_pre is None else up_pre + u
    gate_sig = jax.nn.sigmoid(gate_pre)
    gate_act = gate_pre * gate_sig
    hidden = (gate_act * up_pre).astype(jnp.bfloat16)
    down_grad = lax.psum_scatter(
        lax.dot_general(
            scaled, hidden, (((0,), (0,)), ((), ())), preferred_element_type=jnp.float32
        ).astype(jnp.bfloat16),
        "dp",
        scatter_dimension=0,
        tiled=True,
    )
    grad_w_down = down_grad[None]
    piece_rows = lax.all_gather(w_down, "dp", axis=1, tiled=True)[0]
    out_piece = jnp.dot(hidden, piece_rows.T, preferred_element_type=jnp.float32)
    hidden_grad = jnp.dot(scaled, piece_rows, preferred_element_type=jnp.float32)
    prob_sum = jnp.sum(dy_rows.astype(jnp.float32) * out_piece, axis=1)
    up_grad = (hidden_grad * gate_act).astype(jnp.bfloat16)
    gate_grad = (hidden_grad * up_pre * gate_sig * (1.0 + gate_pre * (1.0 - gate_sig))).astype(
        jnp.bfloat16
    )
    x_grad_rot = jnp.concatenate(
        [
            (
                jnp.dot(gate_grad, piece[0].T, preferred_element_type=jnp.float32)
                + jnp.dot(up_grad, piece[1].T, preferred_element_type=jnp.float32)
            ).astype(jnp.bfloat16)
            for piece in pieces
        ],
        axis=1,
    )
    x_grad = roll_cols(x_grad_rot, -dp_index * shard_rows, model_width)
    prob_block = jnp.zeros((slot_count, lane), jnp.bfloat16).at[:, 0].set(prob_sum.astype(jnp.bfloat16))
    returned = lax.all_to_all(
        jnp.concatenate([x_grad, prob_block], axis=1).reshape(n_expert, capacity, model_width + lane),
        "expert",
        split_axis=0,
        concat_axis=0,
        tiled=True,
    ).reshape(slot_count, model_width + lane)
    grad_slots = returned[:, :model_width]
    prob_slots = returned[:, model_width]
    picked = grad_slots[target].astype(jnp.float32).reshape(tok_count, top_count, model_width)
    grad_x = jnp.sum(picked, axis=1).astype(jnp.bfloat16)
    grad_probs = prob_slots[target].reshape(tok_count, top_count)
    return (grad_x, grad_probs, grad_w_down)


def solution(mesh):
    return jax.shard_map(
        per_device,
        mesh=mesh,
        in_specs=(
            P(("dp", "expert"), None),
            P(("dp", "expert"), None),
            P(("dp", "expert"), None),
            P(("dp", "expert"), None),
            P("expert", "dp", None),
            P("expert", "dp", None),
            P("expert", "dp", None),
        ),
        out_specs=(P(("dp", "expert"), None), P(("dp", "expert"), None), P("expert", "dp", None)),
        check_vma=False,
    )
```

time: 283 us -> 283 us (level); the launches traced: 278 us -> 281 us
  matrix products: 21.2 us -> 52.6 us
  local copies, waits for them, and re-layouts: 55.6 us -> 38.4 us
  starting transfers between devices: 97.7 us -> 83.1 us
    dot_general x5 -> x65, matrix products: 14.4 us -> 47.6 us  [the longest x16 17.1 us: per_device(): g = jnp.dot(cols, piece[0], preferred_element_type=jnp.float32)]
    all_gather x1, waiting for transfers between devices: 0.01 us -> 17.7 us  [per_device(): piece_rows = lax.all_gather(w_down, 'dp', axis=1, tiled=True)[0]]
    ppermute x15, waiting for transfers between devices: 50.2 us -> 33.7 us  [the longest x7 18.5 us: ring_gather_pieces(): b = lax.ppermute(b, axis, bwd)]
    all_to_all x5 -> x2, starting transfers between devices: 40.6 us -> 26.8 us  [the longest x1 15.4 us: per_device(): lax.all_to_all(jnp.concatenate([x_grad, prob_block], axis=1).reshape(n_ex...]
    unnamed x51 -> x118, local copies, waits for them, and re-layouts: 22.4 us -> 8.79 us
    convert_element_type x4 -> x0, local copies, waits for them, and re-layouts: 6.91 us -> none  [the longest x1 3.59 us: per_device(): (p_rows[:, None] * dy_rows.astype(jnp.float32)).astype(jnp.bfloat16)]
    convert_element_type x3 -> x0, other arithmetic: 3.38 us -> none  [the longest x1 3.31 us: per_device(): (p_rows[:, None] * dy_rows.astype(jnp.float32)).astype(jnp.bfloat16)]
    all_to_all x5 -> x2, waiting for transfers between devices: 28.2 us -> 29.8 us  [the longest x1 29.7 us: per_device(): lax.all_to_all(jnp.concatenate([x_grad, prob_block], axis=1).reshape(n_ex...]
  transfers between devices with their start and end apart: 22 -> 19, of which waited for: 9 -> 14; matrix products, arithmetic and copies ran while one was open for 30% -> 22% of each run, Pallas kernels for 0% -> 0%
where the time goes in v3:
time: 283 us; the launch traced here: 281 us
  starting transfers between devices  83.1 us (29%)
  waiting for transfers between devices  81.2 us (29%)
  matrix products  52.6 us (19%)
  local copies, waits for them, and re-layouts  38.4 us (14%)
  between operations  15.4 us (5%)
  other arithmetic  10.8 us (4%)
    ppermute x7, starting transfers between devices, ring_gather_pieces(): b = lax.ppermute(b, axis, bwd)  40.5 us
    all_to_all x1, waiting for transfers between devices, per_device(): lax.all_to_all(jnp.concatenate([x_grad, prob_block], axis=1).reshape(n_ex...  29.7 us
    ppermute x7, waiting for transfers between devices, ring_gather_pieces(): b = lax.ppermute(b, axis, bwd)  18.5 us
    all_gather x1, waiting for transfers between devices, per_device(): piece_rows = lax.all_gather(w_down, 'dp', axis=1, tiled=True)[0]  17.7 us
    dot_general x16, matrix products, per_device(): g = jnp.dot(cols, piece[0], preferred_element_type=jnp.float32)  17.1 us
    ppermute x8, starting transfers between devices, ring_gather_pieces(): f = lax.ppermute(f, axis, fwd)  15.7 us
    all_to_all x1, starting transfers between devices, per_device(): lax.all_to_all(jnp.concatenate([x_grad, prob_block], axis=1).reshape(n_ex...  15.4 us
    ppermute x8, waiting for transfers between devices, ring_gather_pieces(): f = lax.ppermute(f, axis, fwd)  15.2 us
  transfers between devices with their start and end apart: 19, of which 14 were waited for; matrix products, arithmetic and copies ran while one was open for 22% of the time, Pallas kernels for 0%

profile of v3, /device:TPU:1, one launch (start us, length us, event | category | flops | bytes accessed | tf_op | source)
XLA Modules:
  0.0 281.4 jit_solution(10996440502683567129)
XLA Ops:
  10.8 1.4 scatter_custom_fusion
  14.4 3.0 %gather_fusion = bf16[320,2048]{1,0:T(8,128)(2,1)} fusion(bf16[129,2048]{1,0:T(8,128)(2,1)S(1)} %concatenate.28, s32[1024]{0:T(1024)S(1)} %get-tuple-element.68), kind=kCustom, calls=%fused_computation | custom fusion | bytes 2622720 | tf_op jit(solution)/shard_map/gather | solution.py:56
  17.4 3.0 %gather_fusion.1 = bf16[320,2048]{1,0:T(8,128)(2,1)} fusion(bf16[129,2048]{1,0:T(8,128)(2,1)S(1)} %concatenate.29, s32[1024]{0:T(1024)S(1)} %get-tuple-element.68), kind=kCustom, calls=%fused_computation.1 | custom fusion | bytes 2622720 | tf_op jit(solution)/shard_map/gather | solution.py:56
  20.7 2.5 gather_fusion.2
  24.0 1.9 fusion.8
  25.9 2.8 %reshape.148 = bf16[32,10,4224]{2,1,0:T(8,128)(2,1)} reshape(bf16[320,4224]{1,0:T(8,128)(2,1)S(1)} %fusion.8) | data formatting | bytes 5406720 | tf_op jit(solution)/shard_map/reshape | solution.py:58
  28.7 11.4 %all-to-all-start = ((bf16[32,10,4224]{2,1,0:T(8,128)(2,1)}), bf16[32,10,4224]{2,1,0:T(8,128)(2,1)}, u32[]{:S(2)}, u32[]{:S(2)}) async-start(bf16[32,10,4224]{2,1,0:T(8,128)(2,1)} %reshape.148), calls=%async_computation | async-start | bytes 8650752 | tf_op jit(solution)/shard_map/all_to_all | solution.py:57
  40.3 8.5 %collective-permute-start = (bf16[2,128,768]{2,1,0:T(8,128)(2,1)S(1)}, bf16[2,128,768]{2,1,0:T(8,128)(2,1)S(1)}, u32[]{:S(2)}, u32[]{:S(2)}) collective-permute-start(bf16[2,128,768]{2,1,0:T(8,128)(2,1)S(1)} %constant_dynamic-update-slice_fusion), channel_id=1, source_target_pairs={{0,480},{32,0},{64,32},{96,64},{128,96},{160,128},{192,160},{224,1... | collective-permute-start | bytes 1179656 | tf_op jit(solution)/shard_map/ppermute | solution.py:21
  48.7 1.9 collective-permute-start.7
  50.7 6.2 %collective-permute-done = bf16[2,128,768]{2,1,0:T(8,128)(2,1)S(1)} collective-permute-done((bf16[2,128,768]{2,1,0:T(8,128)(2,1)S(1)}, bf16[2,128,768]{2,1,0:T(8,128)(2,1)S(1)}, u32[]{:S(2)}, u32[]{:S(2)}) %collective-permute-start) | collective-permute-done | bytes 393248 | tf_op jit(solution)/shard_map/ppermute | solution.py:21
  56.9 5.4 %collective-permute-start.1 = (bf16[2,128,768]{2,1,0:T(8,128)(2,1)S(1)}, bf16[2,128,768]{2,1,0:T(8,128)(2,1)S(1)}, u32[]{:S(2)}, u32[]{:S(2)}) collective-permute-start(bf16[2,128,768]{2,1,0:T(8,128)(2,1)S(1)} %collective-permute-done), channel_id=1, source_target_pairs={{0,480},{32,0},{64,32},{96,64},{128,96},{160,128},{192,160},{224,1... | collective-permute-start | bytes 1179656 | tf_op jit(solution)/shard_map/ppermute | solution.py:21
  63.1 1.9 collective-permute-start.8
  65.0 4.7 %collective-permute-done.1 = bf16[2,128,768]{2,1,0:T(8,128)(2,1)S(1)} collective-permute-done((bf16[2,128,768]{2,1,0:T(8,128)(2,1)S(1)}, bf16[2,128,768]{2,1,0:T(8,128)(2,1)S(1)}, u32[]{:S(2)}, u32[]{:S(2)}) %collective-permute-start.1) | collective-permute-done | bytes 393248 | tf_op jit(solution)/shard_map/ppermute | solution.py:21
  69.7 5.4 %collective-permute-start.2 = (bf16[2,128,768]{2,1,0:T(8,128)(2,1)S(1)}, bf16[2,128,768]{2,1,0:T(8,128)(2,1)S(1)}, u32[]{:S(2)}, u32[]{:S(2)}) collective-permute-start(bf16[2,128,768]{2,1,0:T(8,128)(2,1)S(1)} %collective-permute-done.1), channel_id=1, source_target_pairs={{0,480},{32,0},{64,32},{96,64},{128,96},{160,128},{192,160},{224,1... | collective-permute-start | bytes 1179656 | tf_op jit(solution)/shard_map/ppermute | solution.py:21
  76.4 1.9 collective-permute-start.9
  78.3 3.5 %collective-permute-done.2 = bf16[2,128,768]{2,1,0:T(8,128)(2,1)S(1)} collective-permute-done((bf16[2,128,768]{2,1,0:T(8,128)(2,1)S(1)}, bf16[2,128,768]{2,1,0:T(8,128)(2,1)S(1)}, u32[]{:S(2)}, u32[]{:S(2)}) %collective-permute-start.2) | collective-permute-done | bytes 393248 | tf_op jit(solution)/shard_map/ppermute | solution.py:21
  81.8 5.4 %collective-permute-start.3 = (bf16[2,128,768]{2,1,0:T(8,128)(2,1)S(1)}, bf16[2,128,768]{2,1,0:T(8,128)(2,1)S(1)}, u32[]{:S(2)}, u32[]{:S(2)}) collective-permute-start(bf16[2,128,768]{2,1,0:T(8,128)(2,1)S(1)} %collective-permute-done.2), channel_id=1, source_target_pairs={{0,480},{32,0},{64,32},{96,64},{128,96},{160,128},{192,160},{224,1... | collective-permute-start | bytes 1179656 | tf_op jit(solution)/shard_map/ppermute | solution.py:21
  88.9 1.9 collective-permute-start.10
  90.8 2.3 collective-permute-done.3
  93.1 5.3 %collective-permute-start.4 = (bf16[2,128,768]{2,1,0:T(8,128)(2,1)S(1)}, bf16[2,128,768]{2,1,0:T(8,128)(2,1)S(1)}, u32[]{:S(2)}, u32[]{:S(2)}) collective-permute-start(bf16[2,128,768]{2,1,0:T(8,128)(2,1)S(1)} %collective-permute-done.3), channel_id=1, source_target_pairs={{0,480},{32,0},{64,32},{96,64},{128,96},{160,128},{192,160},{224,1... | collective-permute-start | bytes 1179656 | tf_op jit(solution)/shard_map/ppermute | solution.py:21
  98.5 1.4 collective-permute-done.10
  100.6 1.9 collective-permute-start.11
  103.5 5.3 %collective-permute-start.5 = (bf16[2,128,768]{2,1,0:T(8,128)(2,1)S(1)}, bf16[2,128,768]{2,1,0:T(8,128)(2,1)}, u32[]{:S(2)}, u32[]{:S(2)}) collective-permute-start(bf16[2,128,768]{2,1,0:T(8,128)(2,1)S(1)} %collective-permute-done.4), channel_id=1, source_target_pairs={{0,480},{32,0},{64,32},{96,64},{128,96},{160,128},{192,160},{224,1... | collective-permute-start | bytes 1179656 | tf_op jit(solution)/shard_map/ppermute | solution.py:21
  108.8 1.9 collective-permute-done.11
  110.7 1.9 collective-permute-start.12
  113.5 5.1 %collective-permute-start.6 = (bf16[2,128,768]{2,1,0:T(8,128)(2,1)}, bf16[2,128,768]{2,1,0:T(8,128)(2,1)}, u32[]{:S(2)}, u32[]{:S(2)}) collective-permute-start(bf16[2,128,768]{2,1,0:T(8,128)(2,1)} %collective-permute-done.5), channel_id=1, source_target_pairs={{0,480},{32,0},{64,32},{96,64},{128,96},{160,128},{192,160},{224,1... | collective-permute-start | bytes 1179656 | tf_op jit(solution)/shard_map/ppermute | solution.py:21
  118.7 1.9 collective-permute-done.12
  120.5 2.1 collective-permute-start.13
  122.7 3.4 %reshape.149 = bf16[320,4224]{1,0:T(8,128)(2,1)S(1)} reshape(bf16[32,10,4224]{2,1,0:T(8,128)(2,1)} %all-to-all-done) | data formatting | bytes 5406720 | tf_op jit(solution)/shard_map/reshape | solution.py:63
  126.1 1.5 copy-done
  145.9 2.1 collective-permute-start.14
  149.2 2.2 convolution_add_fusion.1
  151.4 2.2 fusion.77
  154.8 8.7 %collective-permute-done.14 = bf16[2,128,768]{2,1,0:T(8,128)(2,1)S(1)} collective-permute-done((bf16[2,128,768]{2,1,0:T(8,128)(2,1)}, bf16[2,128,768]{2,1,0:T(8,128)(2,1)S(1)}, u32[]{:S(2)}, u32[]{:S(2)}) %collective-permute-start.14) | collective-permute-done | bytes 393248 | tf_op jit(solution)/shard_map/ppermute | solution.py:18
  163.5 1.5 fusion.26
  165.0 17.7 %all-gather.2.cloned.1.call-done = bf16[1,2048,768]{2,1,0:T(8,128)(2,1)} async-done(((bf16[1,128,768]{2,1,0:T(8,128)(2,1)}), bf16[1,2048,768]{2,1,0:T(8,128)(2,1)}) %all-gather.2.cloned.1.call-update) | async-done | bytes 3145744 | tf_op jit(solution)/shard_map/all_gather | solution.py:93
  182.7 3.7 %fusion.3 = f32[320,768]{1,0:T(8,128)S(1)} fusion(bf16[1,2048,768]{2,1,0:T(8,128)(2,1)} %all-gather.2.cloned.1.call-done, f32[320]{0:T(512)S(1)} %convert_reduce_fusion, bf16[320,4224]{1,0:T(8,128)(2,1)} %copy-done), kind=kOutput, calls=%fused_computation.13 | convolution fusion | flops 1008599040 | bytes 5440768 | tf_op jit(solution)/shard_map/dot_general | solution.py:95
  187.0 2.4 multiply_convert_fusion.1
  190.2 3.6 %convolution_convert_fusion = bf16[2048,768]{1,0:T(8,128)(2,1)} fusion(bf16[320,768]{1,0:T(8,128)(2,1)S(1)} %get-tuple-element.32, f32[320]{0:T(512)S(1)} %convert_reduce_fusion, bf16[320,4224]{1,0:T(8,128)(2,1)S(1)} %copy-done.1), kind=kOutput, calls=%fused_computation.8 | convolution fusion | flops 1010171904 | bytes 4950016 | tf_op jit(solution)/shard_map/dot_general | solution.py:85
  197.9 1.4 fusion.61
  215.6 1.6 reshape.151
  217.2 15.4 %all-to-all-start.1 = ((bf16[32,10,2176]{2,1,0:T(8,128)(2,1)}), bf16[32,10,2176]{2,1,0:T(8,128)(2,1)S(1)}, u32[]{:S(2)}, u32[]{:S(2)}) async-start(bf16[32,10,2176]{2,1,0:T(8,128)(2,1)} %reshape.151), calls=%async_computation.1 | async-start | bytes 4456448 | tf_op jit(solution)/shard_map/all_to_all | solution.py:113
  232.6 29.7 %all-to-all-done.1 = bf16[32,10,2176]{2,1,0:T(8,128)(2,1)S(1)} async-done(((bf16[32,10,2176]{2,1,0:T(8,128)(2,1)}), bf16[32,10,2176]{2,1,0:T(8,128)(2,1)S(1)}, u32[]{:S(2)}, u32[]{:S(2)}) %all-to-all-start.1) | async-done | bytes 1392672 | tf_op jit(solution)/shard_map/all_to_all | solution.py:113
  262.3 1.4 reshape.152
  263.7 1.4 slice.330
  265.1 1.4 gather_fusion.3
  267.2 3.6 %reduce_sum.35 = bf16[128,2048]{1,0:T(8,128)(2,1)} reduce(bf16[128,2,2048]{2,1,0:T(2,128)(2,1)S(1)} %gather.21, bf16[]{:T(256)} %constant.95.clone.1), dimensions={1}, to_apply=%region_6.7 | reduce | flops 262144 | bytes 1572866 | tf_op jit(solution)/shard_map/reduce_sum | solution.py:123
  271.8 1.9 gather_fusion.4
  (227 shorter events, 57.3 us)
Async XLA Ops:
  17.4 3.0 %copy-start.49 = (f32[128,2]{0,1:T(2,128)S(1)}, f32[128,2]{0,1:T(2,128)}, u32[]{:S(2)}) copy-start(f32[128,2]{0,1:T(2,128)} %param.14) | copy-start | bytes 3076
  28.7 11.5 %copy-start.10 = (bf16[1,128,768]{2,1,0:T(8,128)(2,1)S(1)}, bf16[1,128,768]{2,1,0:T(8,128)(2,1)}, u32[]{:S(2)}) copy-start(bf16[1,128,768]{2,1,0:T(8,128)(2,1)} %param.15) | copy-start | bytes 589828
  28.7 11.5 %copy-start.11 = (bf16[1,128,768]{2,1,0:T(8,128)(2,1)S(1)}, bf16[1,128,768]{2,1,0:T(8,128)(2,1)}, u32[]{:S(2)}) copy-start(bf16[1,128,768]{2,1,0:T(8,128)(2,1)} %param.16) | copy-start | bytes 589828
  28.7 93.9 %all-to-all-start = ((bf16[32,10,4224]{2,1,0:T(8,128)(2,1)}), bf16[32,10,4224]{2,1,0:T(8,128)(2,1)}, u32[]{:S(2)}, u32[]{:S(2)}) async-start(bf16[32,10,4224]{2,1,0:T(8,128)(2,1)} %reshape.148), calls=%async_computation | async-start | bytes 8650752 | tf_op jit(solution)/shard_map/all_to_all | solution.py:57
  40.1 142.5 %all-gather.2.cloned.1.call-start = ((), (), s32[]{:S(2)}) async-start(), calls=%async_computation.3 | async-start | bytes 3342336 | tf_op jit(solution)/shard_map/all_gather | solution.py:93
  40.3 16.6 %collective-permute-start = (bf16[2,128,768]{2,1,0:T(8,128)(2,1)S(1)}, bf16[2,128,768]{2,1,0:T(8,128)(2,1)S(1)}, u32[]{:S(2)}, u32[]{:S(2)}) collective-permute-start(bf16[2,128,768]{2,1,0:T(8,128)(2,1)S(1)} %constant_dynamic-update-slice_fusion), channel_id=1, source_target_pairs={{0,480},{32,0},{64,32},{96,64},{128,96},{160,128},{192,160},{224,1... | collective-permute-start | bytes 1179656 | tf_op jit(solution)/shard_map/ppermute | solution.py:21
  48.7 13.6 %collective-permute-start.7 = (bf16[2,128,768]{2,1,0:T(8,128)(2,1)S(1)}, bf16[2,128,768]{2,1,0:T(8,128)(2,1)S(1)}, u32[]{:S(2)}, u32[]{:S(2)}) collective-permute-start(bf16[2,128,768]{2,1,0:T(8,128)(2,1)S(1)} %constant_dynamic-update-slice_fusion), channel_id=1, source_target_pairs={{0,32},{32,64},{64,96},{96,128},{128,160},{160,192},{192,224},{224... | collective-permute-start | bytes 1179656 | tf_op jit(solution)/shard_map/ppermute | solution.py:18
  56.9 53.8 %copy-start.28 = (bf16[2,128,768]{2,1,0:T(8,128)(2,1)}, bf16[2,128,768]{2,1,0:T(8,128)(2,1)S(1)}, u32[]{:S(2)}) copy-start(bf16[2,128,768]{2,1,0:T(8,128)(2,1)S(1)} %collective-permute-done) | copy-start | bytes 1179652
  56.9 12.8 %collective-permute-start.1 = (bf16[2,128,768]{2,1,0:T(8,128)(2,1)S(1)}, bf16[2,128,768]{2,1,0:T(8,128)(2,1)S(1)}, u32[]{:S(2)}, u32[]{:S(2)}) collective-permute-start(bf16[2,128,768]{2,1,0:T(8,128)(2,1)S(1)} %collective-permute-done), channel_id=1, source_target_pairs={{0,480},{32,0},{64,32},{96,64},{128,96},{160,128},{192,160},{224,1... | collective-permute-start | bytes 1179656 | tf_op jit(solution)/shard_map/ppermute | solution.py:21
  63.1 12.5 %collective-permute-start.8 = (bf16[2,128,768]{2,1,0:T(8,128)(2,1)S(1)}, bf16[2,128,768]{2,1,0:T(8,128)(2,1)S(1)}, u32[]{:S(2)}, u32[]{:S(2)}) collective-permute-start(bf16[2,128,768]{2,1,0:T(8,128)(2,1)S(1)} %collective-permute-done.7), channel_id=1, source_target_pairs={{0,32},{32,64},{64,96},{96,128},{128,160},{160,192},{192,224},{224... | collective-permute-start | bytes 1179656 | tf_op jit(solution)/shard_map/ppermute | solution.py:18
  69.7 41.0 %copy-start.31 = (bf16[2,128,768]{2,1,0:T(8,128)(2,1)}, bf16[2,128,768]{2,1,0:T(8,128)(2,1)S(1)}, u32[]{:S(2)}) copy-start(bf16[2,128,768]{2,1,0:T(8,128)(2,1)S(1)} %collective-permute-done.1) | copy-start | bytes 1179652
  69.7 12.1 %collective-permute-start.2 = (bf16[2,128,768]{2,1,0:T(8,128)(2,1)S(1)}, bf16[2,128,768]{2,1,0:T(8,128)(2,1)S(1)}, u32[]{:S(2)}, u32[]{:S(2)}) collective-permute-start(bf16[2,128,768]{2,1,0:T(8,128)(2,1)S(1)} %collective-permute-done.1), channel_id=1, source_target_pairs={{0,480},{32,0},{64,32},{96,64},{128,96},{160,128},{192,160},{224,1... | collective-permute-start | bytes 1179656 | tf_op jit(solution)/shard_map/ppermute | solution.py:21
  76.4 11.8 %collective-permute-start.9 = (bf16[2,128,768]{2,1,0:T(8,128)(2,1)S(1)}, bf16[2,128,768]{2,1,0:T(8,128)(2,1)S(1)}, u32[]{:S(2)}, u32[]{:S(2)}) collective-permute-start(bf16[2,128,768]{2,1,0:T(8,128)(2,1)S(1)} %collective-permute-done.8), channel_id=1, source_target_pairs={{0,32},{32,64},{64,96},{96,128},{128,160},{160,192},{192,224},{224... | collective-permute-start | bytes 1179656 | tf_op jit(solution)/shard_map/ppermute | solution.py:18
  81.8 28.9 %copy-start.34 = (bf16[2,128,768]{2,1,0:T(8,128)(2,1)}, bf16[2,128,768]{2,1,0:T(8,128)(2,1)S(1)}, u32[]{:S(2)}) copy-start(bf16[2,128,768]{2,1,0:T(8,128)(2,1)S(1)} %collective-permute-done.2) | copy-start | bytes 1179652
  81.8 11.3 %collective-permute-start.3 = (bf16[2,128,768]{2,1,0:T(8,128)(2,1)S(1)}, bf16[2,128,768]{2,1,0:T(8,128)(2,1)S(1)}, u32[]{:S(2)}, u32[]{:S(2)}) collective-permute-start(bf16[2,128,768]{2,1,0:T(8,128)(2,1)S(1)} %collective-permute-done.2), channel_id=1, source_target_pairs={{0,480},{32,0},{64,32},{96,64},{128,96},{160,128},{192,160},{224,1... | collective-permute-start | bytes 1179656 | tf_op jit(solution)/shard_map/ppermute | solution.py:21
  88.9 10.9 %collective-permute-start.10 = (bf16[2,128,768]{2,1,0:T(8,128)(2,1)S(1)}, bf16[2,128,768]{2,1,0:T(8,128)(2,1)S(1)}, u32[]{:S(2)}, u32[]{:S(2)}) collective-permute-start(bf16[2,128,768]{2,1,0:T(8,128)(2,1)S(1)} %collective-permute-done.9), channel_id=1, source_target_pairs={{0,32},{32,64},{64,96},{96,128},{128,160},{160,192},{192,224},{224... | collective-permute-start | bytes 1179656 | tf_op jit(solution)/shard_map/ppermute | solution.py:18
  93.1 29.5 %copy-start.37 = (bf16[2,128,768]{2,1,0:T(8,128)(2,1)}, bf16[2,128,768]{2,1,0:T(8,128)(2,1)S(1)}, u32[]{:S(2)}) copy-start(bf16[2,128,768]{2,1,0:T(8,128)(2,1)S(1)} %collective-permute-done.3) | copy-start | bytes 1179652
  93.1 10.4 %collective-permute-start.4 = (bf16[2,128,768]{2,1,0:T(8,128)(2,1)S(1)}, bf16[2,128,768]{2,1,0:T(8,128)(2,1)S(1)}, u32[]{:S(2)}, u32[]{:S(2)}) collective-permute-start(bf16[2,128,768]{2,1,0:T(8,128)(2,1)S(1)} %collective-permute-done.3), channel_id=1, source_target_pairs={{0,480},{32,0},{64,32},{96,64},{128,96},{160,128},{192,160},{224,1... | collective-permute-start | bytes 1179656 | tf_op jit(solution)/shard_map/ppermute | solution.py:21
  100.6 10.1 %collective-permute-start.11 = (bf16[2,128,768]{2,1,0:T(8,128)(2,1)S(1)}, bf16[2,128,768]{2,1,0:T(8,128)(2,1)S(1)}, u32[]{:S(2)}, u32[]{:S(2)}) collective-permute-start(bf16[2,128,768]{2,1,0:T(8,128)(2,1)S(1)} %collective-permute-done.10), channel_id=1, source_target_pairs={{0,32},{32,64},{64,96},{96,128},{128,160},{160,192},{192,224},{224... | collective-permute-start | bytes 1179656 | tf_op jit(solution)/shard_map/ppermute | solution.py:18
  103.5 19.1 %copy-start.41 = (bf16[2,128,768]{2,1,0:T(8,128)(2,1)}, bf16[2,128,768]{2,1,0:T(8,128)(2,1)S(1)}, u32[]{:S(2)}) copy-start(bf16[2,128,768]{2,1,0:T(8,128)(2,1)S(1)} %collective-permute-done.4) | copy-start | bytes 1179652
  103.5 10.0 %collective-permute-start.5 = (bf16[2,128,768]{2,1,0:T(8,128)(2,1)S(1)}, bf16[2,128,768]{2,1,0:T(8,128)(2,1)}, u32[]{:S(2)}, u32[]{:S(2)}) collective-permute-start(bf16[2,128,768]{2,1,0:T(8,128)(2,1)S(1)} %collective-permute-done.4), channel_id=1, source_target_pairs={{0,480},{32,0},{64,32},{96,64},{128,96},{160,128},{192,160},{224,1... | collective-permute-start | bytes 1179656 | tf_op jit(solution)/shard_map/ppermute | solution.py:21
  110.7 12.0 %copy-start.25 = (bf16[2,128,768]{2,1,0:T(8,128)(2,1)}, bf16[2,128,768]{2,1,0:T(8,128)(2,1)S(1)}, u32[]{:S(2)}) copy-start(bf16[2,128,768]{2,1,0:T(8,128)(2,1)S(1)} %collective-permute-done.11) | copy-start | bytes 1179652
  110.7 9.8 %collective-permute-start.12 = (bf16[2,128,768]{2,1,0:T(8,128)(2,1)S(1)}, bf16[2,128,768]{2,1,0:T(8,128)(2,1)}, u32[]{:S(2)}, u32[]{:S(2)}) collective-permute-start(bf16[2,128,768]{2,1,0:T(8,128)(2,1)S(1)} %collective-permute-done.11), channel_id=1, source_target_pairs={{0,32},{32,64},{64,96},{96,128},{128,160},{160,192},{192,224},{224... | collective-permute-start | bytes 1179656 | tf_op jit(solution)/shard_map/ppermute | solution.py:18
  112.7 161.9 %reduce-scatter.2.cloned.1.call-start = ((), (), s32[]{:S(2)}) async-start(), calls=%async_computation.4 | async-start | bytes 3342336 | tf_op jit(solution)/shard_map/reduce_scatter | solution.py:84
  113.5 35.7 %collective-permute-start.6 = (bf16[2,128,768]{2,1,0:T(8,128)(2,1)}, bf16[2,128,768]{2,1,0:T(8,128)(2,1)}, u32[]{:S(2)}, u32[]{:S(2)}) collective-permute-start(bf16[2,128,768]{2,1,0:T(8,128)(2,1)} %collective-permute-done.5), channel_id=1, source_target_pairs={{0,480},{32,0},{64,32},{96,64},{128,96},{160,128},{192,160},{224,1... | collective-permute-start | bytes 1179656 | tf_op jit(solution)/shard_map/ppermute | solution.py:21
  120.5 25.3 %collective-permute-start.13 = (bf16[2,128,768]{2,1,0:T(8,128)(2,1)}, bf16[2,128,768]{2,1,0:T(8,128)(2,1)}, u32[]{:S(2)}, u32[]{:S(2)}) collective-permute-start(bf16[2,128,768]{2,1,0:T(8,128)(2,1)} %collective-permute-done.12), channel_id=1, source_target_pairs={{0,32},{32,64},{64,96},{96,128},{128,160},{160,192},{192,224},{224... | collective-permute-start | bytes 1179656 | tf_op jit(solution)/shard_map/ppermute | solution.py:18
  127.7 2.6 copy-start.26
  131.7 5.0 %copy-start.29 = (bf16[2,128,768]{2,1,0:T(8,128)(2,1)S(1)}, bf16[2,128,768]{2,1,0:T(8,128)(2,1)}, u32[]{:S(2)}) copy-start(bf16[2,128,768]{2,1,0:T(8,128)(2,1)} %copy-done.28) | copy-start | bytes 1179652
  134.2 2.7 copy-start.32
  145.9 17.6 %collective-permute-start.14 = (bf16[2,128,768]{2,1,0:T(8,128)(2,1)}, bf16[2,128,768]{2,1,0:T(8,128)(2,1)S(1)}, u32[]{:S(2)}, u32[]{:S(2)}) collective-permute-start(bf16[2,128,768]{2,1,0:T(8,128)(2,1)} %collective-permute-done.13), channel_id=1, source_target_pairs={{0,32},{32,64},{64,96},{96,128},{128,160},{160,192},{192,224},{224... | collective-permute-start | bytes 1179656 | tf_op jit(solution)/shard_map/ppermute | solution.py:18
  182.6 3.7 %copy-start.3 = (f32[320,768]{1,0:T(8,128)S(1)}, f32[320,768]{1,0:T(8,128)}, u32[]{:S(2)}) copy-start(f32[320,768]{1,0:T(8,128)} %fusion.79) | copy-start | bytes 2949124
  182.6 3.7 %copy-start.4 = (f32[320,768]{1,0:T(8,128)S(1)}, f32[320,768]{1,0:T(8,128)}, u32[]{:S(2)}) copy-start(f32[320,768]{1,0:T(8,128)} %fusion.80) | copy-start | bytes 2949124
  182.6 3.7 %copy-start.5 = (f32[320,768]{1,0:T(8,128)S(1)}, f32[320,768]{1,0:T(8,128)}, u32[]{:S(2)}) copy-start(f32[320,768]{1,0:T(8,128)} %fusion.81) | copy-start | bytes 2949124
  182.6 3.7 %copy-start.6 = (f32[320,768]{1,0:T(8,128)S(1)}, f32[320,768]{1,0:T(8,128)}, u32[]{:S(2)}) copy-start(f32[320,768]{1,0:T(8,128)} %fusion.82) | copy-start | bytes 2949124
  182.6 3.7 %copy-start.7 = (f32[320,768]{1,0:T(8,128)S(1)}, f32[320,768]{1,0:T(8,128)}, u32[]{:S(2)}) copy-start(f32[320,768]{1,0:T(8,128)} %fusion.83) | copy-start | bytes 2949124
  182.7 4.0 %copy-start.8 = (f32[320,768]{1,0:T(8,128)S(1)}, f32[320,768]{1,0:T(8,128)}, u32[]{:S(2)}) copy-start(f32[320,768]{1,0:T(8,128)} %convolution_add_fusion.1) | copy-start | bytes 2949124
  182.7 4.3 %copy-start.9 = (f32[320,768]{1,0:T(8,128)S(1)}, f32[320,768]{1,0:T(8,128)}, u32[]{:S(2)}) copy-start(f32[320,768]{1,0:T(8,128)} %fusion.77) | copy-start | bytes 2949124
  187.0 3.2 %copy-start.1 = (bf16[320,4224]{1,0:T(8,128)(2,1)S(1)}, bf16[320,4224]{1,0:T(8,128)(2,1)}, u32[]{:S(2)}) copy-start(bf16[320,4224]{1,0:T(8,128)(2,1)} %copy-done) | copy-start | bytes 8110084
  195.3 3.9 %copy-start.45 = (bf16[2,128,768]{2,1,0:T(8,128)(2,1)S(1)}, bf16[2,128,768]{2,1,0:T(8,128)(2,1)}, u32[]{:S(2)}) copy-start(bf16[2,128,768]{2,1,0:T(8,128)(2,1)} %copy-done.44) | copy-start | bytes 1179652
  196.3 6.0 %copy-start.27 = (bf16[2,128,768]{2,1,0:T(8,128)(2,1)S(1)}, bf16[2,128,768]{2,1,0:T(8,128)(2,1)}, u32[]{:S(2)}) copy-start(bf16[2,128,768]{2,1,0:T(8,128)(2,1)} %copy-done.25) | copy-start | bytes 1179652
  196.6 6.0 %copy-start.24 = (bf16[2,128,768]{2,1,0:T(8,128)(2,1)S(1)}, bf16[2,128,768]{2,1,0:T(8,128)(2,1)}, u32[]{:S(2)}) copy-start(bf16[2,128,768]{2,1,0:T(8,128)(2,1)} %copy-done.22) | copy-start | bytes 1179652
  197.8 5.0 %copy-start.21 = (bf16[2,128,768]{2,1,0:T(8,128)(2,1)S(1)}, bf16[2,128,768]{2,1,0:T(8,128)(2,1)}, u32[]{:S(2)}) copy-start(bf16[2,128,768]{2,1,0:T(8,128)(2,1)} %copy-done.19) | copy-start | bytes 1179652
  197.9 5.9 %copy-start.48 = (bf16[1,2048,768]{2,1,0:T(8,128)(2,1)S(1)}, bf16[1,2048,768]{2,1,0:T(8,128)(2,1)}, u32[]{:S(2)}) copy-start(bf16[1,2048,768]{2,1,0:T(8,128)(2,1)} %all-gather.2.cloned.1.call-done) | copy-start | bytes 9437188
  199.2 3.9 %copy-start.18 = (bf16[2,128,768]{2,1,0:T(8,128)(2,1)S(1)}, bf16[2,128,768]{2,1,0:T(8,128)(2,1)}, u32[]{:S(2)}) copy-start(bf16[2,128,768]{2,1,0:T(8,128)(2,1)} %copy-done.16) | copy-start | bytes 1179652
  199.6 3.9 %copy-start.15 = (bf16[2,128,768]{2,1,0:T(8,128)(2,1)S(1)}, bf16[2,128,768]{2,1,0:T(8,128)(2,1)}, u32[]{:S(2)}) copy-start(bf16[2,128,768]{2,1,0:T(8,128)(2,1)} %copy-done.13) | copy-start | bytes 1179652
  200.8 2.9 %copy-start.2 = (bf16[320,4224]{1,0:T(8,128)(2,1)S(1)}, bf16[320,4224]{1,0:T(8,128)(2,1)}, u32[]{:S(2)}) copy-start(bf16[320,4224]{1,0:T(8,128)(2,1)} %copy-done) | copy-start | bytes 8110084
  200.8 2.9 %copy-start.47 = (bf16[320,768]{1,0:T(8,128)(2,1)S(1)}, bf16[320,768]{1,0:T(8,128)(2,1)}, u32[]{:S(2)}) copy-start(bf16[320,768]{1,0:T(8,128)(2,1)} %copy-done.46) | copy-start | bytes 1474564
  217.2 45.2 %all-to-all-start.1 = ((bf16[32,10,2176]{2,1,0:T(8,128)(2,1)}), bf16[32,10,2176]{2,1,0:T(8,128)(2,1)S(1)}, u32[]{:S(2)}, u32[]{:S(2)}) async-start(bf16[32,10,2176]{2,1,0:T(8,128)(2,1)} %reshape.151), calls=%async_computation.1 | async-start | bytes 4456448 | tf_op jit(solution)/shard_map/all_to_all | solution.py:113
  (21 other events, 29.2 us)
Sparse Core Ops, SparseCore 0:
  112.8 69.8 all-gather.1
  194.0 71.3 reduce-scatter.1
